TPU v7x, 256 devices: a whole 4x4x8 slice. The times are simulated.
256 devices in a mesh: dp: 64 (over x, z, core), pipe: 4 (over y).
Axes of the slice: x: 4, y: 4, z: 8, core: 2. Of those that a mesh axis runs over, the one named last changes fastest.
Arguments:
- tokens: bfloat16 [8192, 2560], P('dp'), may hold values from -6 to 6
- norm_gains: bfloat16 [4, 2560], P('pipe', 'dp'), may hold values from 0.099609375 to 1.8984375
- up_weights: bfloat16 [4, 64, 128, 128], P('pipe', 'dp'), may hold values from -0.5 to 0.5
- down_weights: bfloat16 [4, 64, 128, 128], P('pipe', 'dp'), may hold values from -0.3125 to 0.3125
- coords: int32 [4, 4, 64], P('pipe'), may hold values from 0 to 79, as said below
- cotangent: bfloat16 [8192, 2560], P('dp'), may hold values from -6 to 6
Outputs:
- grad_up: float32 [4, 64, 128, 128], P('pipe', 'dp')
- grad_down: float32 [4, 64, 128, 128], P('pipe', 'dp')
- grad_gain: float32 [4, 2560], P('pipe', 'dp')
- grad_inputs: bfloat16 [4, 8192, 2560], P('pipe', 'dp')
Inputs may be any that keep to these rules, and one draw needn't show every extreme that they name: For every layer the 64 pairs (coords[l,0,b], coords[l,1,b]) are distinct, and so are the pairs (coords[l,2,b], coords[l,3,b]); rows 0 and 3 lie below 20, rows 1 and 2 below 80.
All inputs are finite; a program needn't handle non-finite values.
Results may differ from a plain program's by a relative error of at most 0.011.
Values may be sent and summed in bfloat16 or wider, within the bound.
No kernel may reach another device: no remote copies, remote signals or barrier semaphores. Data moves between devices by JAX's collectives and lax.ppermute only.
A program may use at most 128 MiB of HBM per device.

v0:
```python
import math

import jax
import jax.numpy as jnp
from jax import lax
from jax.sharding import PartitionSpec as P

FF = 10240
MICRO = 8


epsilon = 1e-05


def from_behind(value, axis, by):
    size = lax.axis_size(axis)
    pairs = [(i, i + by) for i in range(size) if 0 <= i + by < size]
    return lax.ppermute(value, axis, pairs)


def norm_parts(inputs, gain_row):
    widened = inputs.astype(jnp.float32)
    inverse = lax.rsqrt(jnp.mean(widened * widened, axis=-1, keepdims=True) + epsilon)
    unit_rows = widened * inverse
    normed = (unit_rows * gain_row.astype(jnp.float32)).astype(jnp.bfloat16)
    return (widened, inverse, unit_rows, normed)


def to_panels(values, panel_width):
    row_count = values.shape[0]
    return jnp.transpose(values.reshape(row_count, -1, panel_width), (1, 0, 2))


def from_panels(panels):
    return jnp.transpose(panels, (1, 0, 2)).reshape(
        panels.shape[1], panels.shape[0] * panels.shape[2]
    )


def panel_product(panels, blocks, pick_index, put_index, put_count, form):
    picked = jnp.take(panels, pick_index, axis=0)
    products = jnp.einsum(form, picked, blocks, preferred_element_type=jnp.float32)
    placing = (put_index[:, None] == jnp.arange(put_count, dtype=jnp.int32)[None, :]).astype(
        jnp.float32
    )
    return jnp.einsum("brc,bp->prc", products, placing, precision=lax.Precision.HIGHEST)


def up_product(inputs, gain_row, up_blocks, block_links, hidden_panels, panel_width):
    normed = norm_parts(inputs, gain_row)[3]
    return panel_product(
        to_panels(normed, panel_width),
        up_blocks,
        block_links[0],
        block_links[1],
        hidden_panels,
        "bri,bio->bro",
    )


def layer_forward(
    inputs, gain_row, up_blocks, down_blocks, block_links, hidden_panels, model_panels, panel_width
):
    widened, inverse, unit_rows, normed = norm_parts(inputs, gain_row)
    before = panel_product(
        to_panels(normed, panel_width),
        up_blocks,
        block_links[0],
        block_links[1],
        hidden_panels,
        "bri,bio->bro",
    )
    active = jax.nn.gelu(before).astype(jnp.bfloat16)
    added = from_panels(
        panel_product(
            active, down_blocks, block_links[2], block_links[3], model_panels, "bri,bio->bro"
        )
    )
    return ((widened + added).astype(jnp.bfloat16), before)


def layer_backward(
    inputs,
    upstream,
    before,
    gain_row,
    up_blocks,
    down_blocks,
    block_links,
    hidden_panels,
    model_panels,
    panel_width,
):
    widened, inverse, unit_rows, normed = norm_parts(inputs, gain_row)
    upstream_panels = to_panels(upstream, panel_width)
    active_full, gelu_slope = jax.jvp(jax.nn.gelu, (before,), (jnp.ones_like(before),))
    active = active_full.astype(jnp.bfloat16)
    grad_active = panel_product(
        upstream_panels, down_blocks, block_links[3], block_links[2], hidden_panels, "bro,bio->bri"
    )
    grad_before = (grad_active * gelu_slope).astype(jnp.bfloat16)
    grad_normed = from_panels(
        panel_product(
            grad_before, up_blocks, block_links[1], block_links[0], model_panels, "bro,bio->bri"
        )
    )
    gain_grad = jnp.sum(grad_normed * unit_rows, axis=0)
    grad_unit = grad_normed * gain_row.astype(jnp.float32)
    centered = grad_unit - unit_rows * jnp.mean(grad_unit * unit_rows, axis=-1, keepdims=True)
    grad_local = (upstream.astype(jnp.float32) + inverse * centered).astype(jnp.bfloat16)
    return (
        grad_local,
        gain_grad,
        to_panels(normed, panel_width),
        active,
        grad_before,
        upstream_panels,
    )


def own_slots(collected, first):
    stacked = jnp.stack(collected)
    return lax.dynamic_slice_in_dim(stacked, first, MICRO, 0)


def shards(tokens, norm_gains, up_weights, down_weights, coords, cotangent):
    phases = lax.axis_size("pipe")
    section = lax.axis_index("pipe")
    panel_width = up_weights.shape[2]
    model_width = tokens.shape[1]
    token_rows = tokens.shape[0]
    hidden_panels = FF // panel_width
    model_panels = model_width // panel_width
    group_rows = token_rows // MICRO
    block_links = coords[0]
    gathered = (
        lax.all_gather(up_weights, "dp", axis=1, tiled=True),
        lax.all_gather(down_weights, "dp", axis=1, tiled=True),
        lax.all_gather(norm_gains, "dp", axis=1, tiled=True),
    )
    up_blocks = gathered[0][0]
    down_blocks = gathered[1][0]
    gain_row = gathered[2][0]
    token_groups = tokens.reshape(MICRO, group_rows, model_width)
    cot_groups = cot_groups_of = cotangent.reshape(MICRO, group_rows, model_width)
    last_tick = MICRO + phases - 2
    input_list = []
    arriving = jnp.zeros((group_rows, model_width), jnp.bfloat16)
    for moment in range(last_tick + 1):
        current = jnp.where(section == 0, token_groups[min(moment, MICRO - 1)], arriving)
        input_list.append(current)
        leaving, before = layer_forward(
            current,
            gain_row,
            up_blocks,
            down_blocks,
            block_links,
            hidden_panels,
            model_panels,
            panel_width,
        )
        if moment < last_tick:
            arriving = from_behind(leaving, "pipe", 1)
    input_stack = jnp.stack(input_list)
    gain_total = jnp.zeros((model_width,), jnp.float32)
    grad_list = []
    normed_list = []
    upper_list = []
    active_list = []
    slope_list = []
    arriving = jnp.zeros((group_rows, model_width), jnp.bfloat16)
    for moment in range(last_tick + 1):
        slot_index = moment - (phases - 1 - section)
        slot_live = (slot_index >= 0) & (slot_index < MICRO)
        tick_place = jnp.clip(slot_index, 0, MICRO - 1) + section
        upstream = jnp.where(section == phases - 1, cot_groups_of[min(moment, MICRO - 1)], arriving)
        inputs = lax.dynamic_index_in_dim(input_stack, tick_place, 0, keepdims=False)
        before = up_product(inputs, gain_row, up_blocks, block_links, hidden_panels, panel_width)
        grad_local, gain_grad, normed, active, grad_before, upper = layer_backward(
            inputs,
            upstream,
            before,
            gain_row,
            up_blocks,
            down_blocks,
            block_links,
            hidden_panels,
            model_panels,
            panel_width,
        )
        gain_total = gain_total + jnp.where(slot_live, gain_grad, 0.0)
        grad_list.append(grad_local)
        normed_list.append(normed)
        upper_list.append(upper)
        active_list.append(active)
        slope_list.append(grad_before)
        if moment < last_tick:
            arriving = from_behind(grad_local, "pipe", -1)
    first = phases - 1 - section
    grad_store = own_slots(grad_list, first)
    normed_all = own_slots(normed_list, first)
    upper_all = own_slots(upper_list, first)
    active_all = own_slots(active_list, first)
    slope_all = own_slots(slope_list, first)
    grad_scale = 1.0 / math.sqrt(token_rows * lax.axis_size("dp"))
    up_total = jnp.einsum(
        "mbri,mbro->bio",
        jnp.take(normed_all, block_links[0], axis=1),
        jnp.take(slope_all, block_links[1], axis=1),
        preferred_element_type=jnp.float32,
    )
    down_total = jnp.einsum(
        "mbri,mbro->bio",
        jnp.take(active_all, block_links[2], axis=1),
        jnp.take(upper_all, block_links[3], axis=1),
        preferred_element_type=jnp.float32,
    )
    summed = (
        lax.psum_scatter(up_total[None], "dp", scatter_dimension=1, tiled=True),
        lax.psum_scatter(down_total[None], "dp", scatter_dimension=1, tiled=True),
        lax.psum_scatter(gain_total[None], "dp", scatter_dimension=1, tiled=True),
    )
    up_out = summed[0]
    down_out = summed[1]
    gain_out = summed[2]
    return (
        up_out * grad_scale,
        down_out * grad_scale,
        gain_out * grad_scale,
        grad_store.reshape(1, token_rows, model_width),
    )


def solution(mesh):
    in_specs = (
        P("dp", None),
        P("pipe", "dp"),
        P("pipe", "dp", None, None),
        P("pipe", "dp", None, None),
        P("pipe", None, None),
        P("dp", None),
    )
    out_specs = (
        P("pipe", "dp", None, None),
        P("pipe", "dp", None, None),
        P("pipe", "dp"),
        P("pipe", "dp", None),
    )
    return jax.shard_map(shards, mesh=mesh, in_specs=in_specs, out_specs=out_specs, check_vma=False)
```

profile of v0, /device:TPU:8, one launch (start us, length us, event | category | flops | bytes accessed | tf_op | source)
XLA Modules:
  0.0 850.1 jit_solution(10716014187815840585)
XLA Ops:
  12.6 133.8 %all-reduce = bf16[2560]{0:T(1024)(128)(2,1)S(1)} all-reduce(bf16[2560]{0:T(1024)(128)(2,1)S(1)} %dynamic-update-slice), channel_id=1, replica_groups=mesh['dp'=64,'pipe'=4] {'dp'}, use_global_device_ids=true, to_apply=%add | all-reduce | flops 2560 | bytes 10240
  151.7 2.3 fusion.108
  155.6 13.2 %all-gather.5.cloned.1.call-done = bf16[1,64,128,128]{3,2,0,1:T(8,128)(2,1)} async-done(((bf16[1,1,128,128]{3,2,0,1:T(8,128)(2,1)}), bf16[1,64,128,128]{3,2,0,1:T(8,128)(2,1)}) %all-gather.5.cloned.1.call-update) | async-done | bytes 2097168 | tf_op jit(solution)/shard_map/all_gather | solution.py:138
  168.8 2.4 fusion.44
  171.7 3.5 collective-permute-start
  184.5 2.3 gather_fusion.3
  186.8 2.4 fusion.42
  189.7 3.4 collective-permute-start.1
  193.7 2.3 collective-permute-done.1
  201.6 2.5 gather_fusion.5
  204.1 2.4 fusion.40
  207.0 3.6 collective-permute-start.2
  219.8 2.5 gather_fusion.7
  222.3 2.4 fusion.38
  225.2 3.4 collective-permute-start.3
  229.2 2.3 collective-permute-done.3
  238.0 2.5 gather_fusion.9
  240.4 2.4 fusion.36
  243.3 3.4 collective-permute-start.4
  247.4 2.3 collective-permute-done.4
  256.1 2.5 gather_fusion.11
  258.6 2.4 fusion.34
  261.5 3.4 collective-permute-start.5
  265.6 2.3 collective-permute-done.5
  274.3 2.5 gather_fusion.13
  276.8 2.4 fusion.32
  279.7 3.8 collective-permute-start.6
  292.5 2.5 gather_fusion.15
  294.9 2.4 fusion.30
  297.8 3.4 collective-permute-start.7
  301.9 2.3 collective-permute-done.7
  310.7 2.5 gather_fusion.17
  313.1 2.4 fusion.28
  316.0 3.4 collective-permute-start.8
  320.1 2.3 collective-permute-done.8
  328.8 2.5 gather_fusion.19
  331.3 2.4 fusion.26
  334.2 3.6 collective-permute-start.9
  342.1 2.2 fusion.624
  364.5 2.9 fusion.22
  367.4 2.3 bitcast_dynamic-update-slice_fusion.20
  379.9 2.4 bitcast_dynamic-update-slice_fusion.8
  383.7 2.9 fusion.20
  386.6 2.3 bitcast_dynamic-update-slice_fusion.19
  398.8 2.4 bitcast_dynamic-update-slice_fusion.7
  402.6 2.9 fusion.18
  405.5 2.3 bitcast_dynamic-update-slice_fusion.18
  414.2 2.3 collective-permute-start.13
  421.4 2.9 fusion.16
  439.7 2.9 fusion.14
  458.0 2.9 fusion.12
  476.3 2.9 fusion.10
  494.6 2.9 fusion.8
  512.8 2.9 fusion.6
  530.3 2.3 gather_fusion.20
  534.3 2.9 fusion.4
  543.1 4.0 gather_fusion.53
  547.1 5.2 convolution_bitcast_fusion.1
  556.4 2.2 copy.177
  558.6 4.2 gather_fusion.54
  566.2 2.4 gather_fusion.55
  568.6 5.3 convolution_bitcast_fusion
  580.5 246.6 %all-reduce.1 = f32[1,2560]{1,0:T(1,128)S(1)} all-reduce(f32[1,2560]{1,0:T(1,128)S(1)} %bitcast.1085), channel_id=4, replica_groups=mesh['dp'=64,'pipe'=4] {'dp'}, use_global_device_ids=true, to_apply=%region_44.49.clone | all-reduce | flops 2560 | bytes 20480
  832.8 8.9 %reduce-scatter.6.cloned.1.call-done = f32[1,1,128,128]{3,2,1,0:T(8,128)} async-done(((f32[1,64,128,128]{3,2,1,0:T(8,128)}), f32[1,1,128,128]{3,2,1,0:T(8,128)}) %reduce-scatter.6.cloned.1.call-update) | async-done | bytes 65552 | tf_op jit(solution)/shard_map/reduce_scatter | solution.py:220
  (536 shorter events, 262.5 us)
Async XLA Ops:
  7.2 143.9 %copy-start.5 = (bf16[128,2560]{1,0:T(8,128)(2,1)S(1)}, bf16[128,2560]{1,0:T(8,128)(2,1)}, u32[]{:S(2)}) copy-start(bf16[128,2560]{1,0:T(8,128)(2,1)} %param.14) | copy-start | bytes 1966084
  7.2 143.9 %copy-start.65 = (s32[1,4,64]{2,1,0:T(4,128)S(1)}, s32[1,4,64]{2,1,0:T(4,128)}, u32[]{:S(2)}) copy-start(s32[1,4,64]{2,1,0:T(4,128)} %param.18) | copy-start | bytes 3076
  7.2 141.9 %copy-start.2 = (bf16[128,2560]{1,0:T(8,128)(2,1)S(1)}, bf16[128,2560]{1,0:T(8,128)(2,1)}, u32[]{:S(2)}) copy-start(bf16[128,2560]{1,0:T(8,128)(2,1)} %param.19) | copy-start | bytes 1966084
  7.2 144.5 %all-gather.3.cloned.1.call-start = ((), (), s32[]{:S(2)}) async-start(), calls=%async_computation.2 | async-start | bytes 2129920 | tf_op jit(solution)/shard_map/all_gather | solution.py:137
  7.9 160.8 %all-gather.5.cloned.1.call-start = ((), (), s32[]{:S(2)}) async-start(), calls=%async_computation.3 | async-start | bytes 2129920 | tf_op jit(solution)/shard_map/all_gather | solution.py:138
  8.7 822.7 %reduce-scatter.4.cloned.1.call-start = ((), (), s32[]{:S(2)}) async-start(), calls=%async_computation.4 | async-start | bytes 4259840 | tf_op jit(solution)/shard_map/reduce_scatter | solution.py:219
  148.5 30.8 %copy-start.44 = (s32[1024]{0:T(1024)}, s32[1024]{0:T(1024)S(1)}, u32[]{:S(2)}) copy-start(s32[1024]{0:T(1024)S(1)} %get-tuple-element.166) | copy-start | bytes 12292
  148.5 202.5 %copy-start.55 = (s32[1024]{0:T(1024)}, s32[1024]{0:T(1024)S(1)}, u32[]{:S(2)}) copy-start(s32[1024]{0:T(1024)S(1)} %get-tuple-element.165) | copy-start | bytes 12292
  149.2 35.3 %copy-start.59 = (s32[1024]{0:T(1024)}, s32[1024]{0:T(1024)S(1)}, u32[]{:S(2)}) copy-start(s32[1024]{0:T(1024)S(1)} %get-tuple-element.168) | copy-start | bytes 12292
  151.1 198.1 %copy-start.69 = (s32[64]{0:T(128)}, s32[64]{0:T(128)S(1)}, u32[]{:S(2)}) copy-start(s32[64]{0:T(128)S(1)} %get-tuple-element.101) | copy-start | bytes 772
  168.8 6.5 copy-start.1
  168.8 6.5 copy-start.24
  171.7 8.9 %copy-start = (bf16[1,64,128,128]{3,2,0,1:T(8,128)(2,1)S(1)}, bf16[1,64,128,128]{3,2,0,1:T(8,128)(2,1)}, u32[]{:S(2)}) copy-start(bf16[1,64,128,128]{3,2,0,1:T(8,128)(2,1)} %all-gather.3.cloned.1.call-done) | copy-start | bytes 6291460
  171.7 6.6 collective-permute-start
  184.5 5.2 copy-start.7
  189.6 10.3 %copy-start.75 = (s32[64]{0:T(128)S(1)}, s32[64]{0:T(128)}, u32[]{:S(2)}) copy-start(s32[64]{0:T(128)} %copy-done.74) | copy-start | bytes 772
  189.7 6.3 collective-permute-start.1
  201.6 5.3 copy-start.11
  207.0 6.3 collective-permute-start.2
  219.8 5.3 copy-start.13
  225.2 6.3 collective-permute-start.3
  238.0 5.3 copy-start.15
  243.3 6.3 collective-permute-start.4
  256.1 5.3 copy-start.17
  261.5 6.3 collective-permute-start.5
  274.3 5.3 copy-start.19
  279.7 6.3 collective-permute-start.6
  292.5 5.3 copy-start.21
  297.8 6.3 collective-permute-start.7
  310.7 5.3 copy-start.23
  316.0 6.3 collective-permute-start.8
  328.8 5.3 copy-start.9
  333.7 12.6 %copy-start.45 = (s32[1024]{0:T(1024)S(1)}, s32[1024]{0:T(1024)}, u32[]{:S(2)}) copy-start(s32[1024]{0:T(1024)} %copy-done.44) | copy-start | bytes 12292
  334.2 6.3 collective-permute-start.9
  345.6 14.3 %copy-start.63 = (f32[16]{0:T(128)}, f32[16]{0:T(128)S(1)}, u32[]{:S(2)}) copy-start(f32[16]{0:T(128)S(1)} %add_rsqrt_fusion.9) | copy-start | bytes 196
  356.1 7.7 collective-permute-start.10
  371.1 7.3 copy-start.60
  376.2 6.8 collective-permute-start.11
  383.0 10.6 %copy-start.25 = (bf16[16,2560]{1,0:T(8,128)(2,1)}, bf16[16,2560]{1,0:T(8,128)(2,1)S(1)}, u32[]{:S(2)}) copy-start(bf16[16,2560]{1,0:T(8,128)(2,1)S(1)} %collective-permute-done.11) | copy-start | bytes 245764
  395.4 6.5 collective-permute-start.12
  401.9 10.6 %copy-start.27 = (bf16[16,2560]{1,0:T(8,128)(2,1)}, bf16[16,2560]{1,0:T(8,128)(2,1)S(1)}, u32[]{:S(2)}) copy-start(bf16[16,2560]{1,0:T(8,128)(2,1)S(1)} %collective-permute-done.12) | copy-start | bytes 245764
  414.2 6.5 collective-permute-start.13
  419.8 4.5 copy-start.70
  420.7 10.1 %copy-start.29 = (bf16[16,2560]{1,0:T(8,128)(2,1)}, bf16[16,2560]{1,0:T(8,128)(2,1)S(1)}, u32[]{:S(2)}) copy-start(bf16[16,2560]{1,0:T(8,128)(2,1)S(1)} %collective-permute-done.13) | copy-start | bytes 245764
  432.5 6.5 collective-permute-start.14
  437.7 4.9 copy-start.71
  439.0 10.0 %copy-start.31 = (bf16[16,2560]{1,0:T(8,128)(2,1)}, bf16[16,2560]{1,0:T(8,128)(2,1)S(1)}, u32[]{:S(2)}) copy-start(bf16[16,2560]{1,0:T(8,128)(2,1)S(1)} %collective-permute-done.14) | copy-start | bytes 245764
  450.8 6.5 collective-permute-start.15
  456.1 4.8 copy-start.72
  457.3 10.0 %copy-start.33 = (bf16[16,2560]{1,0:T(8,128)(2,1)}, bf16[16,2560]{1,0:T(8,128)(2,1)S(1)}, u32[]{:S(2)}) copy-start(bf16[16,2560]{1,0:T(8,128)(2,1)S(1)} %collective-permute-done.15) | copy-start | bytes 245764
  469.1 6.5 collective-permute-start.16
  475.6 10.0 %copy-start.35 = (bf16[16,2560]{1,0:T(8,128)(2,1)}, bf16[16,2560]{1,0:T(8,128)(2,1)S(1)}, u32[]{:S(2)}) copy-start(bf16[16,2560]{1,0:T(8,128)(2,1)S(1)} %collective-permute-done.16) | copy-start | bytes 245764
  487.3 6.5 collective-permute-start.17
  493.9 10.0 %copy-start.37 = (bf16[16,2560]{1,0:T(8,128)(2,1)}, bf16[16,2560]{1,0:T(8,128)(2,1)S(1)}, u32[]{:S(2)}) copy-start(bf16[16,2560]{1,0:T(8,128)(2,1)S(1)} %collective-permute-done.17) | copy-start | bytes 245764
  505.6 6.6 collective-permute-start.18
  512.2 10.0 %copy-start.39 = (bf16[16,2560]{1,0:T(8,128)(2,1)}, bf16[16,2560]{1,0:T(8,128)(2,1)S(1)}, u32[]{:S(2)}) copy-start(bf16[16,2560]{1,0:T(8,128)(2,1)S(1)} %collective-permute-done.18) | copy-start | bytes 245764
  518.8 7.3 copy-start.66
  523.9 8.7 %collective-permute-start.19 = (bf16[16,2560]{1,0:T(8,128)(2,1)}, bf16[16,2560]{1,0:T(8,128)(2,1)}, u32[]{:S(2)}, u32[]{:S(2)}) collective-permute-start(bf16[16,2560]{1,0:T(8,128)(2,1)} %get-tuple-element.42), channel_id=1, source_target_pairs={{1,0},{2,1},{3,2},{5,4},{6,5},{7,6},{9,8},{10,9},{11,10},{13,12},{... | collective-permute-start | bytes 245768 | tf_op jit(solution)/shard_map/ppermute | solution.py:18
  532.6 4.6 copy-start.73
  552.4 289.3 %reduce-scatter.6.cloned.1.call-start = ((), (), s32[]{:S(2)}) async-start(), calls=%async_computation.5 | async-start | bytes 4259840 | tf_op jit(solution)/shard_map/reduce_scatter | solution.py:220
  574.0 5.7 copy-start.4
  574.0 5.7 copy-start.67
  575.8 4.5 copy-start.46
  575.9 4.5 copy-start.47
  (51 other events, 115.8 us)
Sparse Core Ops, SparseCore 0:
  10.8 80.0 all-gather.2
  93.7 75.0 all-gather.4
  552.5 142.5 reduce-scatter.3
  699.6 142.0 reduce-scatter.5
where the time goes:
time: 861 us; the launch traced here: 850 us
  blocking collectives  380 us (44%)
  matrix products  180 us (21%)
  local copies, waits for them, and re-layouts  116 us (13%)
  starting transfers between devices  55.6 us (6%)
  other arithmetic  53.1 us (6%)
  waiting for transfers between devices  47.3 us (5%)
  between operations  17.6 us (2%)
    unnamed x2, blocking collectives  380 us
    dot_general x53, matrix products, panel_product(): jnp.einsum(form, picked, blocks, preferred_element_type=jnp.float32)  104 us
    dot_general x53, matrix products, panel_product(): jnp.einsum('brc,bp->prc', products, placing, precision=lax.Precision.HIGH...  66 us
    gather x53, local copies, waits for them, and re-layouts, panel_product(): picked = jnp.take(panels, pick_index, axis=0)  65.6 us
    ppermute x20, starting transfers between devices, from_behind(): return lax.ppermute(value, axis, pairs)  55.4 us
    unnamed x32, other arithmetic  26 us
    ppermute x20, waiting for transfers between devices, from_behind(): return lax.ppermute(value, axis, pairs)  23.9 us
  transfers between devices with their start and end apart: 24, of which 18 were waited for; matrix products, arithmetic and copies ran while one was open for 11% of the time, Pallas kernels for 0%

commit v1 on v0

--- a/solution.py
+++ b/solution.py
@@ -6,7 +6,7 @@
 from jax.sharding import PartitionSpec as P
 
 FF = 10240
-MICRO = 8
+MICRO = 2
 
 
 epsilon = 1e-05
@@ -133,14 +133,24 @@
     model_panels = model_width // panel_width
     group_rows = token_rows // MICRO
     block_links = coords[0]
-    gathered = (
-        lax.all_gather(up_weights, "dp", axis=1, tiled=True),
-        lax.all_gather(down_weights, "dp", axis=1, tiled=True),
-        lax.all_gather(norm_gains, "dp", axis=1, tiled=True),
-    )
-    up_blocks = gathered[0][0]
-    down_blocks = gathered[1][0]
-    gain_row = gathered[2][0]
+    block_width = panel_width * panel_width
+    gain_count = norm_gains.shape[1]
+    gain_room = -(-gain_count // 128) * 128
+    packed = jnp.concatenate(
+        [
+            up_weights.reshape(1, 1, block_width),
+            down_weights.reshape(1, 1, block_width),
+            jnp.pad(norm_gains.reshape(1, 1, gain_count), ((0, 0), (0, 0), (0, gain_room - gain_count))),
+        ],
+        axis=2,
+    )
+    gathered = lax.all_gather(packed, "dp", axis=1, tiled=True)[0]
+    block_count = gathered.shape[0]
+    up_blocks = gathered[:, :block_width].reshape(block_count, panel_width, panel_width)
+    down_blocks = gathered[:, block_width : 2 * block_width].reshape(
+        block_count, panel_width, panel_width
+    )
+    gain_row = gathered[:, 2 * block_width : 2 * block_width + gain_count].reshape(-1)
     token_groups = tokens.reshape(MICRO, group_rows, model_width)
     cot_groups = cot_groups_of = cotangent.reshape(MICRO, group_rows, model_width)
     last_tick = MICRO + phases - 2
@@ -215,18 +225,27 @@
         jnp.take(upper_all, block_links[3], axis=1),
         preferred_element_type=jnp.float32,
     )
-    summed = (
-        lax.psum_scatter(up_total[None], "dp", scatter_dimension=1, tiled=True),
-        lax.psum_scatter(down_total[None], "dp", scatter_dimension=1, tiled=True),
-        lax.psum_scatter(gain_total[None], "dp", scatter_dimension=1, tiled=True),
-    )
-    up_out = summed[0]
-    down_out = summed[1]
-    gain_out = summed[2]
+    gain_parts = jnp.pad(
+        gain_total.reshape(block_count, gain_count), ((0, 0), (0, 8 * 128 - gain_count))
+    )
+    totals = jnp.concatenate(
+        [
+            up_total.reshape(block_count, block_width),
+            down_total.reshape(block_count, block_width),
+            gain_parts,
+        ],
+        axis=1,
+    )
+    summed = lax.psum_scatter(
+        totals.reshape(1, block_count, -1, 128), "dp", scatter_dimension=1, tiled=True
+    ).reshape(-1) * grad_scale
+    up_out = summed[:block_width].reshape(1, 1, panel_width, panel_width)
+    down_out = summed[block_width : 2 * block_width].reshape(1, 1, panel_width, panel_width)
+    gain_out = summed[2 * block_width : 2 * block_width + gain_count].reshape(1, gain_count)
     return (
-        up_out * grad_scale,
-        down_out * grad_scale,
-        gain_out * grad_scale,
+        up_out,
+        down_out,
+        gain_out,
         grad_store.reshape(1, token_rows, model_width),
     )
 

time: 861 us -> 667 us (0.77)
  blocking collectives: 380 us -> 0 us
  waiting for transfers between devices: 47.3 us -> 251 us
  local copies, waits for them, and re-layouts: 116 us -> 152 us
  starting transfers between devices: 55.6 us -> 23.3 us
  matrix products: 180 us -> 163 us
    unnamed x2 -> x0, blocking collectives: 380 us -> none
    unnamed x4 -> x3, waiting for transfers between devices: 1.41 us -> 145 us
    all_gather x2 -> x1, waiting for transfers between devices: 13.2 us -> 79.4 us  [shards(): gathered = lax.all_gather(packed, 'dp', axis=1, tiled=True)[0]]
    dot_general x53 -> x23, matrix products: 104 us -> 60.9 us  [panel_product(): jnp.einsum(form, picked, blocks, preferred_element_type=jnp.float32)]
    ppermute x20 -> x8, starting transfers between devices: 55.4 us -> 23.2 us  [from_behind(): return lax.ppermute(value, axis, pairs)]
    dot_general x53 -> x23, matrix products: 66 us -> 96.2 us  [panel_product(): jnp.einsum('brc,bp->prc', products, placing, precision=lax.Precision.HIGH...]
    unnamed x195 -> x176, local copies, waits for them, and re-layouts: 16.1 us -> 28.9 us
    transpose x32 -> x13, other arithmetic: 3.05 us -> 12 us  [to_panels(): return jnp.transpose(values.reshape(row_count, -1, panel_width), (1, 0, 2))]
  transfers between devices with their start and end apart: 24 -> 10, of which waited for: 18 -> 7; matrix products, arithmetic and copies ran while one was open for 11% -> 10% of each run, Pallas kernels for 0% -> 0%
where the time goes in v1:
time: 667 us; the launch traced here: 657 us
  waiting for transfers between devices  251 us (38%)
  matrix products  163 us (24%)
  local copies, waits for them, and re-layouts  152 us (23%)
  other arithmetic  52.3 us (8%)
  starting transfers between devices  23.3 us (3%)
  between operations  15.4 us (2%)
    unnamed x3, waiting for transfers between devices  145 us
    dot_general x23, matrix products, panel_product(): jnp.einsum('brc,bp->prc', products, placing, precision=lax.Precision.HIGH...  96.2 us
    all_gather x1, waiting for transfers between devices, shards(): gathered = lax.all_gather(packed, 'dp', axis=1, tiled=True)[0]  79.4 us
    gather x23, local copies, waits for them, and re-layouts, panel_product(): picked = jnp.take(panels, pick_index, axis=0)  65.1 us
    dot_general x23, matrix products, panel_product(): jnp.einsum(form, picked, blocks, preferred_element_type=jnp.float32)  60.9 us
    unnamed x176, local copies, waits for them, and re-layouts  28.9 us
    ppermute x8, waiting for transfers between devices, from_behind(): return lax.ppermute(value, axis, pairs)  26.7 us
    ppermute x8, starting transfers between devices, from_behind(): return lax.ppermute(value, axis, pairs)  23.2 us
  transfers between devices with their start and end apart: 10, of which 7 were waited for; matrix products, arithmetic and copies ran while one was open for 10% of the time, Pallas kernels for 0%

profile of v1, /device:TPU:8, one launch (start us, length us, event | category | flops | bytes accessed | tf_op | source)
XLA Modules:
  0.0 656.8 jit_solution(14191049537095383817)
XLA Ops:
  17.8 79.4 %all-gather.2.cloned.1.call-done = bf16[1,64,32896]{2,0,1:T(2,128)(2,1)} async-done(((bf16[1,1,32896]{2,0,1:T(2,128)(2,1)}), bf16[1,64,32896]{2,0,1:T(2,128)(2,1)}) %all-gather.2.cloned.1.call-update) | async-done | bytes 4210704 | tf_op jit(solution)/shard_map/all_gather | solution.py:147
  97.2 3.8 copy.292
  111.6 3.6 fusion.68
  116.7 3.0 gather_fusion.1
  124.5 3.6 collective-permute-start
  128.1 2.9 fusion.199
  131.0 5.3 collective-permute-done
  142.8 3.6 fusion.76
  147.9 3.0 gather_fusion.3
  155.7 3.6 collective-permute-start.1
  160.1 6.5 collective-permute-done.1
  173.1 3.6 fusion.84
  178.2 3.0 gather_fusion.5
  186.0 3.9 collective-permute-start.2
  190.6 5.4 collective-permute-done.2
  202.6 3.6 fusion.92
  207.6 3.0 gather_fusion.7
  215.5 3.5 collective-permute-start.3
  219.8 4.8 collective-permute-done.3
  233.2 2.8 gather_fusion.10
  238.0 4.8 bitcast_dynamic-update-slice_fusion.4
  242.8 6.0 bitcast_dynamic-update-slice_fusion.9
  250.3 3.1 gather_fusion.11
  253.4 2.8 fusion.195
  256.2 4.0 multiply_reduce_fusion
  271.9 2.8 gather_fusion.13
  274.7 3.4 fusion.191
  283.0 2.8 gather_fusion.16
  290.3 5.5 bitcast_dynamic-update-slice_fusion.3
  295.8 5.4 bitcast_dynamic-update-slice_fusion.2
  303.0 2.8 gather_fusion.12
  305.7 3.6 fusion.193
  309.4 6.2 bitcast_dynamic-update-slice_fusion.8
  317.0 3.1 gather_fusion.14
  320.1 2.8 fusion.189
  323.0 3.2 fusion.251
  332.5 4.7 collective-permute-done.5
  341.5 3.6 fusion.187
  345.2 5.9 bitcast_dynamic-update-slice_fusion.7
  352.5 3.1 gather_fusion.17
  355.6 2.8 fusion.183
  358.4 3.2 fusion.248
  366.8 2.7 gather_fusion.19
  375.5 5.4 bitcast_dynamic-update-slice_fusion.1
  385.2 3.6 fusion.181
  388.8 6.0 bitcast_dynamic-update-slice_fusion.6
  396.3 3.1 gather_fusion.20
  399.4 2.8 fusion.177
  402.2 3.2 fusion.245
  410.6 2.7 gather_fusion.22
  417.7 5.5 bitcast_dynamic-update-slice_fusion
  427.3 4.0 gather_fusion.24
  435.1 3.5 gather_fusion.8
  442.1 2.8 gather_fusion.21
  444.9 3.6 fusion.175
  448.6 5.9 bitcast_dynamic-update-slice_fusion.5
  455.9 3.1 gather_fusion.26
  459.0 2.8 fusion.171
  461.9 3.9 fusion.244
  471.2 3.2 fusion.93
  474.4 4.4 copy.293
  482.9 4.2 gather_fusion.23
  492.9 4.9 copy.164
  503.0 144.6 %reduce-scatter.5.cloned.1.call-done = f32[1,1,264,128]{3,2,1,0:T(8,128)} async-done(((f32[1,64,264,128]{3,2,1,0:T(8,128)}), f32[1,1,264,128]{3,2,1,0:T(8,128)}) %reduce-scatter.5.cloned.1.call-update) | async-done | bytes 135184
  (312 shorter events, 178.3 us)
Async XLA Ops:
  7.2 5.3 copy-start.60
  7.2 6.4 copy-start.1
  7.2 90.0 %all-gather.2.cloned.1.call-start = ((), (), s32[]{:S(2)}) async-start(), calls=%async_computation.1 | async-start | bytes 8552960 | tf_op jit(solution)/shard_map/all_gather | solution.py:147
  10.3 637.3 %reduce-scatter.5.cloned.1.call-start = ((), (), s32[]{:S(2)}) async-start(), calls=%async_computation.2 | async-start | bytes 8785920
  11.4 3.9 copy-start.5
  13.0 115.1 %copy-start.38 = (pred[64]{0:T(512)(128)(4,1)}, pred[64]{0:T(512)(128)(4,1)S(1)}, u32[]{:S(2)}) copy-start(pred[64]{0:T(512)(128)(4,1)S(1)} %get-tuple-element.64) | copy-start | bytes 196
  13.0 197.7 %copy-start.46 = (pred[64]{0:T(512)(128)(4,1)}, pred[64]{0:T(512)(128)(4,1)S(1)}, u32[]{:S(2)}) copy-start(pred[64]{0:T(512)(128)(4,1)S(1)} %get-tuple-element.60) | copy-start | bytes 196
  15.4 182.5 %copy-start.40 = (s32[1024]{0:T(1024)}, s32[1024]{0:T(1024)S(1)}, u32[]{:S(2)}) copy-start(s32[1024]{0:T(1024)S(1)} %get-tuple-element.94) | copy-start | bytes 12292
  15.4 192.3 %copy-start.52 = (s32[1024]{0:T(1024)}, s32[1024]{0:T(1024)S(1)}, u32[]{:S(2)}) copy-start(s32[1024]{0:T(1024)S(1)} %get-tuple-element.93) | copy-start | bytes 12292
  16.2 186.4 %copy-start.74 = (s32[64]{0:T(128)}, s32[64]{0:T(128)S(1)}, u32[]{:S(2)}) copy-start(s32[64]{0:T(128)S(1)} %get-tuple-element.57) | copy-start | bytes 772
  102.9 93.4 %copy-start.26 = (f32[2560]{0:T(1024)}, f32[2560]{0:T(1024)S(1)}, u32[]{:S(2)}) copy-start(f32[2560]{0:T(1024)S(1)} %reshape.558) | copy-start | bytes 30724
  122.3 5.8 copy-start
  122.4 5.8 copy-start.15
  124.5 11.8 %collective-permute-start = (bf16[64,2560]{1,0:T(8,128)(2,1)S(1)}, bf16[64,2560]{1,0:T(8,128)(2,1)S(1)}, u32[]{:S(2)}, u32[]{:S(2)}) collective-permute-start(bf16[64,2560]{1,0:T(8,128)(2,1)S(1)} %fusion.287), channel_id=1, source_target_pairs={{0,1},{1,2},{2,3},{4,5},{5,6},{6,7},{8,9},{9,10},{10,11},{12,13},{... | collective-permute-start | bytes 983048 | tf_op jit(solution)/shard_map/ppermute | solution.py:18
  155.7 11.0 %collective-permute-start.1 = (bf16[64,2560]{1,0:T(8,128)(2,1)S(1)}, bf16[64,2560]{1,0:T(8,128)(2,1)S(1)}, u32[]{:S(2)}, u32[]{:S(2)}) collective-permute-start(bf16[64,2560]{1,0:T(8,128)(2,1)S(1)} %fusion.260), channel_id=1, source_target_pairs={{0,1},{1,2},{2,3},{4,5},{5,6},{6,7},{8,9},{9,10},{10,11},{12,13},{... | collective-permute-start | bytes 983048 | tf_op jit(solution)/shard_map/ppermute | solution.py:18
  186.0 10.0 %collective-permute-start.2 = (bf16[64,2560]{1,0:T(8,128)(2,1)S(1)}, bf16[64,2560]{1,0:T(8,128)(2,1)S(1)}, u32[]{:S(2)}, u32[]{:S(2)}) collective-permute-start(bf16[64,2560]{1,0:T(8,128)(2,1)S(1)} %fusion.264), channel_id=1, source_target_pairs={{0,1},{1,2},{2,3},{4,5},{5,6},{6,7},{8,9},{9,10},{10,11},{12,13},{... | collective-permute-start | bytes 983048 | tf_op jit(solution)/shard_map/ppermute | solution.py:18
  215.5 9.1 %collective-permute-start.3 = (bf16[64,2560]{1,0:T(8,128)(2,1)S(1)}, bf16[64,2560]{1,0:T(8,128)(2,1)S(1)}, u32[]{:S(2)}, u32[]{:S(2)}) collective-permute-start(bf16[64,2560]{1,0:T(8,128)(2,1)S(1)} %fusion.268), channel_id=1, source_target_pairs={{0,1},{1,2},{2,3},{4,5},{5,6},{6,7},{8,9},{9,10},{10,11},{12,13},{... | collective-permute-start | bytes 983048 | tf_op jit(solution)/shard_map/ppermute | solution.py:18
  238.0 4.8 copy-start.23
  238.0 4.8 copy-start.69
  253.4 2.8 copy-start.41
  253.4 2.8 copy-start.49
  260.1 4.8 copy-start.63
  262.2 3.8 copy-start.68
  274.6 3.4 copy-start.8
  274.6 3.4 copy-start.27
  274.7 3.4 copy-start.50
  274.7 3.4 copy-start.64
  274.7 7.6 %copy-start.25 = (bf16[20,64,128]{2,0,1:T(8,128)(2,1)S(1)}, bf16[20,64,128]{2,0,1:T(8,128)(2,1)}, u32[]{:S(2)}) copy-start(bf16[20,64,128]{2,0,1:T(8,128)(2,1)} %get-tuple-element.54) | copy-start | bytes 983044
  280.0 21.1 %collective-permute-start.4 = (bf16[64,2560]{1,0:T(8,128)(2,1)}, bf16[64,2560]{1,0:T(8,128)(2,1)}, u32[]{:S(2)}, u32[]{:S(2)}) collective-permute-start(bf16[64,2560]{1,0:T(8,128)(2,1)} %fusion.254), channel_id=1, source_target_pairs={{1,0},{2,1},{3,2},{5,4},{6,5},{7,6},{9,8},{10,9},{11,10},{13,12},{... | collective-permute-start | bytes 983048 | tf_op jit(solution)/shard_map/ppermute | solution.py:18
  285.8 3.6 copy-start.58
  305.7 3.6 copy-start.70
  305.7 3.6 copy-start.81
  320.1 2.8 copy-start.4
  320.1 2.9 copy-start.42
  320.1 2.9 copy-start.62
  323.0 3.2 copy-start.28
  326.2 4.0 copy-start.65
  328.3 9.0 %collective-permute-start.5 = (bf16[64,2560]{1,0:T(8,128)(2,1)S(1)}, bf16[64,2560]{1,0:T(8,128)(2,1)S(1)}, u32[]{:S(2)}, u32[]{:S(2)}) collective-permute-start(bf16[64,2560]{1,0:T(8,128)(2,1)S(1)} %get-tuple-element.28), channel_id=1, source_target_pairs={{1,0},{2,1},{3,2},{5,4},{6,5},{7,6},{9,8},{10,9},{11,10},{13,12},{... | collective-permute-start | bytes 983048 | tf_op jit(solution)/shard_map/ppermute | solution.py:18
  341.5 3.6 copy-start.71
  341.5 3.6 copy-start.79
  355.6 2.8 copy-start.43
  355.6 2.8 copy-start.59
  358.4 3.2 copy-start.21
  358.4 3.2 copy-start.29
  369.6 4.2 copy-start.55
  369.6 5.1 copy-start.22
  371.6 3.9 copy-start.77
  371.6 9.3 %collective-permute-start.6 = (bf16[64,2560]{1,0:T(8,128)(2,1)S(1)}, bf16[64,2560]{1,0:T(8,128)(2,1)S(1)}, u32[]{:S(2)}, u32[]{:S(2)}) collective-permute-start(bf16[64,2560]{1,0:T(8,128)(2,1)S(1)} %copy-done.32), channel_id=1, source_target_pairs={{1,0},{2,1},{3,2},{5,4},{6,5},{7,6},{9,8},{10,9},{11,10},{13,12},{... | collective-permute-start | bytes 983048 | tf_op jit(solution)/shard_map/ppermute | solution.py:18
  385.2 3.6 copy-start.72
  385.2 3.6 copy-start.82
  399.4 2.8 copy-start.56
  402.2 3.2 copy-start.19
  402.2 3.2 copy-start.30
  413.3 4.4 copy-start.78
  415.3 25.1 %collective-permute-start.7 = (bf16[64,2560]{1,0:T(8,128)(2,1)}, bf16[64,2560]{1,0:T(8,128)(2,1)}, u32[]{:S(2)}, u32[]{:S(2)}) collective-permute-start(bf16[64,2560]{1,0:T(8,128)(2,1)} %get-tuple-element.24), channel_id=1, source_target_pairs={{1,0},{2,1},{3,2},{5,4},{6,5},{7,6},{9,8},{10,9},{11,10},{13,12},{... | collective-permute-start | bytes 983048 | tf_op jit(solution)/shard_map/ppermute | solution.py:18
  444.9 3.6 copy-start.73
  444.9 3.6 copy-start.80
  459.0 2.8 copy-start.53
  461.8 4.0 copy-start.33
  461.8 3.9 copy-start.34
  461.8 3.9 copy-start.35
  461.9 3.9 copy-start.36
  482.9 4.2 copy-start.6
  482.9 4.2 copy-start.37
  (29 other events, 48.7 us)
Sparse Core Ops, SparseCore 0:
  11.3 85.8 all-gather.1
  498.0 149.6 reduce-scatter.4

commit v2 on v1

--- a/solution.py
+++ b/solution.py
@@ -43,7 +43,7 @@
     placing = (put_index[:, None] == jnp.arange(put_count, dtype=jnp.int32)[None, :]).astype(
         jnp.float32
     )
-    return jnp.einsum("brc,bp->prc", products, placing, precision=lax.Precision.HIGHEST)
+    return jnp.einsum("brc,bp->prc", products, placing, precision=lax.Precision.HIGH)
 
 
 def up_product(inputs, gain_row, up_blocks, block_links, hidden_panels, panel_width):
@@ -155,6 +155,7 @@
     cot_groups = cot_groups_of = cotangent.reshape(MICRO, group_rows, model_width)
     last_tick = MICRO + phases - 2
     input_list = []
+    before_list = []
     arriving = jnp.zeros((group_rows, model_width), jnp.bfloat16)
     for moment in range(last_tick + 1):
         current = jnp.where(section == 0, token_groups[min(moment, MICRO - 1)], arriving)
@@ -169,9 +170,11 @@
             model_panels,
             panel_width,
         )
+        before_list.append(before)
         if moment < last_tick:
             arriving = from_behind(leaving, "pipe", 1)
     input_stack = jnp.stack(input_list)
+    before_stack = jnp.stack(before_list)
     gain_total = jnp.zeros((model_width,), jnp.float32)
     grad_list = []
     normed_list = []
@@ -185,7 +188,7 @@
         tick_place = jnp.clip(slot_index, 0, MICRO - 1) + section
         upstream = jnp.where(section == phases - 1, cot_groups_of[min(moment, MICRO - 1)], arriving)
         inputs = lax.dynamic_index_in_dim(input_stack, tick_place, 0, keepdims=False)
-        before = up_product(inputs, gain_row, up_blocks, block_links, hidden_panels, panel_width)
+        before = lax.dynamic_index_in_dim(before_stack, tick_place, 0, keepdims=False)
         grad_local, gain_grad, normed, active, grad_before, upper = layer_backward(
             inputs,
             upstream,

time: 667 us -> 636 us (0.954)
  matrix products: 163 us -> 128 us
  other arithmetic: 52.3 us -> 80.1 us
  local copies, waits for them, and re-layouts: 152 us -> 126 us
    dot_general x23 -> x19, matrix products: 96.2 us -> 71.2 us  [panel_product(): jnp.einsum('brc,bp->prc', products, placing, precision=lax.Precision.HIGH)]
    unnamed x13 -> x20, other arithmetic: 17.3 us -> 41 us
    gather x23 -> x19, local copies, waits for them, and re-layouts: 65.1 us -> 49 us  [panel_product(): picked = jnp.take(panels, pick_index, axis=0)]
    dot_general x23 -> x19, matrix products: 60.9 us -> 51.1 us  [panel_product(): jnp.einsum(form, picked, blocks, preferred_element_type=jnp.float32)]
    unnamed x176 -> x131, local copies, waits for them, and re-layouts: 28.9 us -> 28.9 us
  transfers between devices with their start and end apart: 10 -> 10, of which waited for: 7 -> 8; matrix products, arithmetic and copies ran while one was open for 10% -> 11% of each run, Pallas kernels for 0% -> 0%
where the time goes in v2:
time: 636 us; the launch traced here: 627 us
  waiting for transfers between devices  254 us (40%)
  matrix products  128 us (20%)
  local copies, waits for them, and re-layouts  126 us (20%)
  other arithmetic  80.1 us (13%)
  starting transfers between devices  22.9 us (4%)
  between operations  15.2 us (2%)
    unnamed x3, waiting for transfers between devices  146 us
    all_gather x1, waiting for transfers between devices, shards(): gathered = lax.all_gather(packed, 'dp', axis=1, tiled=True)[0]  84.3 us
    dot_general x19, matrix products, panel_product(): jnp.einsum('brc,bp->prc', products, placing, precision=lax.Precision.HIGH)  71.2 us
    dot_general x19, matrix products, panel_product(): jnp.einsum(form, picked, blocks, preferred_element_type=jnp.float32)  51.1 us
    gather x19, local copies, waits for them, and re-layouts, panel_product(): picked = jnp.take(panels, pick_index, axis=0)  49 us
    unnamed x20, other arithmetic  41 us
    unnamed x131, local copies, waits for them, and re-layouts  28.9 us
    ppermute x8, waiting for transfers between devices, from_behind(): return lax.ppermute(value, axis, pairs)  23.9 us
  transfers between devices with their start and end apart: 10, of which 8 were waited for; matrix products, arithmetic and copies ran while one was open for 11% of the time, Pallas kernels for 0%

profile of v2, /device:TPU:8, one launch (start us, length us, event | category | flops | bytes accessed | tf_op | source)
XLA Modules:
  0.0 626.6 jit_solution(7334065427860682173)
XLA Ops:
  12.9 84.3 %all-gather.2.cloned.1.call-done = bf16[1,64,32896]{2,0,1:T(2,128)(2,1)} async-done(((bf16[1,1,32896]{2,0,1:T(2,128)(2,1)}), bf16[1,64,32896]{2,0,1:T(2,128)(2,1)}) %all-gather.2.cloned.1.call-update) | async-done | bytes 4210704 | tf_op jit(solution)/shard_map/all_gather | solution.py:147
  97.2 3.8 copy.258
  109.6 3.5 bitcast_dynamic-update-slice_fusion.4
  117.2 3.0 gather_fusion.1
  120.2 2.6 fusion.238
  124.6 3.9 collective-permute-start
  129.4 7.0 %collective-permute-done = bf16[64,2560]{1,0:T(8,128)(2,1)S(1)} collective-permute-done((bf16[64,2560]{1,0:T(8,128)(2,1)S(1)}, bf16[64,2560]{1,0:T(8,128)(2,1)S(1)}, u32[]{:S(2)}, u32[]{:S(2)}) %collective-permute-start) | collective-permute-done | bytes 327712 | tf_op jit(solution)/shard_map/ppermute | solution.py:18
  141.2 3.5 bitcast_dynamic-update-slice_fusion.3
  147.0 3.0 gather_fusion.3
  150.0 2.6 fusion.234
  155.1 3.6 collective-permute-start.1
  159.5 6.9 %collective-permute-done.1 = bf16[64,2560]{1,0:T(8,128)(2,1)} collective-permute-done((bf16[64,2560]{1,0:T(8,128)(2,1)}, bf16[64,2560]{1,0:T(8,128)(2,1)}, u32[]{:S(2)}, u32[]{:S(2)}) %collective-permute-start.1) | collective-permute-done | bytes 327712 | tf_op jit(solution)/shard_map/ppermute | solution.py:18
  174.4 3.5 bitcast_dynamic-update-slice_fusion.2
  180.2 3.0 gather_fusion.5
  183.2 2.6 fusion.230
  188.3 3.6 collective-permute-start.2
  192.5 2.6 gather_fusion.9
  196.0 2.7 collective-permute-done.2
  202.1 2.6 gather_fusion.6
  206.6 3.6 bitcast_dynamic-update-slice_fusion.1
  212.5 3.0 gather_fusion.7
  215.5 2.6 fusion.226
  219.9 3.6 collective-permute-start.3
  223.5 2.9 fusion.222
  233.8 3.6 bitcast_dynamic-update-slice_fusion
  237.4 3.8 fusion.201
  241.2 6.7 %bitcast_dynamic-update-slice_fusion.9 = (bf16[5,80,64,128]{3,1,2,0:T(8,128)(2,1)}, bf16[80,64,128]{2,0,1:T(8,128)(2,1)S(1)}) fusion(f32[5,80,64,128]{3,1,2,0:T(8,128)} %bitcast_dynamic-update-slice_fusion, s32[]{:T(128)S(6)} %select_n.163, f32[64,64,128]{2,1,0:T(8,128)S(1)} %copy-done.25, s32[64]{0:T(128)S(1)} %get-tuple-element.59), kind=kOutput, calls=%fused_computation.248 | convolution fusion | flops 263459840 | bytes 7340292 | tf_op jit(solution)/shard_map/brc,bp->prc/dot_general | solution.py:46
  255.3 3.1 gather_fusion.11
  258.4 2.8 fusion.218
  262.1 2.8 multiply_reduce_fusion
  271.5 3.2 dynamic-slice_convert_fusion
  281.5 3.7 fusion.200
  285.2 3.7 fusion.199
  288.8 3.8 fusion.198
  294.5 3.7 fusion.197
  302.8 2.7 gather_fusion.12
  305.5 3.5 fusion.216
  309.0 6.9 %bitcast_dynamic-update-slice_fusion.8 = (bf16[5,80,64,128]{3,1,2,0:T(8,128)(2,1)}, bf16[80,64,128]{2,0,1:T(8,128)(2,1)S(1)}) fusion(bf16[5,80,64,128]{3,1,2,0:T(8,128)(2,1)} %get-tuple-element.79, f32[5,80,64,128]{3,1,2,0:T(8,128)} %bitcast_dynamic-update-slice_fusion, s32[]{:T(128)S(6)} %select_n.164, f32[64,64,128]{2,1,0:T(8,128)S(1)} %fusion.216, ...), kind=kOutput, calls=%fused_computation.247 | convolution fusion | flops 263459840 | bytes 7340292 | tf_op jit(solution)/shard_map/brc,bp->prc/dot_general | solution.py:46
  317.3 3.1 gather_fusion.13
  320.4 2.8 fusion.214
  323.2 2.8 fusion.270
  330.2 3.4 constant_dynamic-slice_fusion.2
  339.6 2.7 gather_fusion.14
  342.3 3.5 fusion.212
  345.8 6.9 %bitcast_dynamic-update-slice_fusion.7 = (bf16[5,80,64,128]{3,1,2,0:T(8,128)(2,1)}, bf16[80,64,128]{2,0,1:T(8,128)(2,1)S(1)}) fusion(bf16[5,80,64,128]{3,1,2,0:T(8,128)(2,1)} %get-tuple-element.81, f32[5,80,64,128]{3,1,2,0:T(8,128)} %bitcast_dynamic-update-slice_fusion, s32[]{:T(128)S(6)} %select_n.165, f32[64,64,128]{2,1,0:T(8,128)S(1)} %fusion.212, ...), kind=kOutput, calls=%fused_computation.246 | convolution fusion | flops 263459840 | bytes 7340292 | tf_op jit(solution)/shard_map/brc,bp->prc/dot_general | solution.py:46
  354.1 3.0 gather_fusion.15
  357.1 2.8 fusion.210
  370.1 3.9 copy.116
  374.0 4.0 gather_fusion.20
  382.7 3.5 fusion.208
  386.1 7.1 %bitcast_dynamic-update-slice_fusion.6 = (bf16[5,80,64,128]{3,1,2,0:T(8,128)(2,1)}, bf16[80,64,128]{2,0,1:T(8,128)(2,1)S(1)}) fusion(bf16[5,80,64,128]{3,1,2,0:T(8,128)(2,1)} %get-tuple-element.83, f32[5,80,64,128]{3,1,2,0:T(8,128)} %bitcast_dynamic-update-slice_fusion, s32[]{:T(128)S(6)} %select_n.166, f32[64,64,128]{2,1,0:T(8,128)S(1)} %fusion.208, ...), kind=kOutput, calls=%fused_computation.245 | convolution fusion | flops 263459840 | bytes 7340292 | tf_op jit(solution)/shard_map/brc,bp->prc/dot_general | solution.py:46
  394.6 3.0 gather_fusion.17
  397.6 2.8 fusion.206
  410.4 3.4 collective-permute-done.7
  416.4 3.5 fusion.204
  419.9 6.8 %bitcast_dynamic-update-slice_fusion.5 = (bf16[5,80,64,128]{3,1,2,0:T(8,128)(2,1)}, bf16[80,64,128]{2,0,1:T(8,128)(2,1)S(1)}) fusion(bf16[5,80,64,128]{3,1,2,0:T(8,128)(2,1)} %get-tuple-element.85, f32[5,80,64,128]{3,1,2,0:T(8,128)} %bitcast_dynamic-update-slice_fusion, s32[]{:T(128)S(6)} %select_n.167, f32[64,64,128]{2,1,0:T(8,128)S(1)} %fusion.204, ...), kind=kOutput, calls=%fused_computation.244 | convolution fusion | flops 263459840 | bytes 7340292 | tf_op jit(solution)/shard_map/brc,bp->prc/dot_general | solution.py:46
  428.1 3.0 gather_fusion.22
  431.1 2.8 fusion.202
  441.4 3.2 fusion.136
  444.6 4.4 copy.260
  454.3 4.6 copy.259
  459.0 3.8 fusion
  462.8 4.9 copy.145
  471.6 145.8 %reduce-scatter.5.cloned.1.call-done = f32[1,1,264,128]{3,2,1,0:T(8,128)} async-done(((f32[1,64,264,128]{3,2,1,0:T(8,128)}), f32[1,1,264,128]{3,2,1,0:T(8,128)}) %reduce-scatter.5.cloned.1.call-update) | async-done | bytes 135184
  (261 shorter events, 151.8 us)
Async XLA Ops:
  7.2 4.9 copy-start.2
  7.2 4.3 copy-start.48
  7.2 90.0 %all-gather.2.cloned.1.call-start = ((), (), s32[]{:S(2)}) async-start(), calls=%async_computation.1 | async-start | bytes 8552960 | tf_op jit(solution)/shard_map/all_gather | solution.py:147
  10.3 607.1 %reduce-scatter.5.cloned.1.call-start = ((), (), s32[]{:S(2)}) async-start(), calls=%async_computation.2 | async-start | bytes 8785920
  12.0 203.4 %copy-start.42 = (pred[64]{0:T(512)(128)(4,1)}, pred[64]{0:T(512)(128)(4,1)S(1)}, u32[]{:S(2)}) copy-start(pred[64]{0:T(512)(128)(4,1)S(1)} %get-tuple-element.60) | copy-start | bytes 196
  12.0 219.8 %copy-start.37 = (pred[64]{0:T(512)(128)(4,1)}, pred[64]{0:T(512)(128)(4,1)S(1)}, u32[]{:S(2)}) copy-start(pred[64]{0:T(512)(128)(4,1)S(1)} %get-tuple-element.62) | copy-start | bytes 196
  12.1 200.4 %copy-start.47 = (s32[1024]{0:T(1024)}, s32[1024]{0:T(1024)S(1)}, u32[]{:S(2)}) copy-start(s32[1024]{0:T(1024)S(1)} %get-tuple-element.91) | copy-start | bytes 12292
  12.1 218.1 %copy-start.44 = (s32[1024]{0:T(1024)}, s32[1024]{0:T(1024)S(1)}, u32[]{:S(2)}) copy-start(s32[1024]{0:T(1024)S(1)} %get-tuple-element.92) | copy-start | bytes 12292
  12.9 228.4 %copy-start.58 = (s32[64]{0:T(128)}, s32[64]{0:T(128)S(1)}, u32[]{:S(2)}) copy-start(s32[64]{0:T(128)S(1)} %get-tuple-element.59) | copy-start | bytes 772
  113.1 2.3 copy-start.4
  124.6 11.8 %collective-permute-start = (bf16[64,2560]{1,0:T(8,128)(2,1)S(1)}, bf16[64,2560]{1,0:T(8,128)(2,1)S(1)}, u32[]{:S(2)}, u32[]{:S(2)}) collective-permute-start(bf16[64,2560]{1,0:T(8,128)(2,1)S(1)} %fusion.309), channel_id=1, source_target_pairs={{0,1},{1,2},{2,3},{4,5},{5,6},{6,7},{8,9},{9,10},{10,11},{12,13},{... | collective-permute-start | bytes 983048 | tf_op jit(solution)/shard_map/ppermute | solution.py:18
  129.4 100.6 %copy-start.26 = (f32[2560]{0:T(1024)}, f32[2560]{0:T(1024)S(1)}, u32[]{:S(2)}) copy-start(f32[2560]{0:T(1024)S(1)} %reshape.565) | copy-start | bytes 30724
  137.2 4.0 copy-start.16
  152.6 1.6 copy-start.17
  152.6 6.1 copy-start.1
  155.1 11.3 %collective-permute-start.1 = (bf16[64,2560]{1,0:T(8,128)(2,1)}, bf16[64,2560]{1,0:T(8,128)(2,1)}, u32[]{:S(2)}, u32[]{:S(2)}) collective-permute-start(bf16[64,2560]{1,0:T(8,128)(2,1)} %fusion.282), channel_id=1, source_target_pairs={{0,1},{1,2},{2,3},{4,5},{5,6},{6,7},{8,9},{9,10},{10,11},{12,13},{... | collective-permute-start | bytes 983048 | tf_op jit(solution)/shard_map/ppermute | solution.py:18
  188.3 10.4 %collective-permute-start.2 = (bf16[64,2560]{1,0:T(8,128)(2,1)}, bf16[64,2560]{1,0:T(8,128)(2,1)}, u32[]{:S(2)}, u32[]{:S(2)}) collective-permute-start(bf16[64,2560]{1,0:T(8,128)(2,1)} %fusion.286), channel_id=1, source_target_pairs={{0,1},{1,2},{2,3},{4,5},{5,6},{6,7},{8,9},{9,10},{10,11},{12,13},{... | collective-permute-start | bytes 983048 | tf_op jit(solution)/shard_map/ppermute | solution.py:18
  192.5 12.2 %copy-start.45 = (s32[1024]{0:T(1024)}, s32[1024]{0:T(1024)S(1)}, u32[]{:S(2)}) copy-start(s32[1024]{0:T(1024)S(1)} %get-tuple-element.90) | copy-start | bytes 12292
  218.1 1.6 copy-start.15
  218.1 5.4 copy-start
  218.1 5.4 copy-start.20
  219.9 9.1 %collective-permute-start.3 = (bf16[64,2560]{1,0:T(8,128)(2,1)S(1)}, bf16[64,2560]{1,0:T(8,128)(2,1)S(1)}, u32[]{:S(2)}, u32[]{:S(2)}) collective-permute-start(bf16[64,2560]{1,0:T(8,128)(2,1)S(1)} %fusion.290), channel_id=1, source_target_pairs={{0,1},{1,2},{2,3},{4,5},{5,6},{6,7},{8,9},{9,10},{10,11},{12,13},{... | collective-permute-start | bytes 983048 | tf_op jit(solution)/shard_map/ppermute | solution.py:18
  237.4 3.8 copy-start.25
  258.4 2.8 copy-start.49
  258.4 3.7 copy-start.39
  261.2 4.6 copy-start.27
  265.0 6.5 %copy-start.28 = (f32[2560]{0:T(1024)S(1)}, f32[2560]{0:T(1024)}, u32[]{:S(2)}) copy-start(f32[2560]{0:T(1024)} %copy-done.26) | copy-start | bytes 30724
  265.0 6.5 %copy-start.50 = (f32[64]{0:T(128)S(1)}, f32[64]{0:T(128)}, u32[]{:S(2)}) copy-start(f32[64]{0:T(128)} %add_rsqrt_fusion.5) | copy-start | bytes 772
  267.8 33.1 %collective-permute-start.4 = (bf16[64,2560]{1,0:T(8,128)(2,1)}, bf16[64,2560]{1,0:T(8,128)(2,1)}, u32[]{:S(2)}, u32[]{:S(2)}) collective-permute-start(bf16[64,2560]{1,0:T(8,128)(2,1)} %fusion.276), channel_id=1, source_target_pairs={{1,0},{2,1},{3,2},{5,4},{6,5},{7,6},{9,8},{10,9},{11,10},{13,12},{... | collective-permute-start | bytes 983048 | tf_op jit(solution)/shard_map/ppermute | solution.py:18
  271.5 5.3 copy-start.57
  278.5 15.1 %copy-start.9 = (f32[64,20,128]{2,1,0:T(8,128)}, f32[64,20,128]{2,1,0:T(8,128)S(1)}, u32[]{:S(2)}) copy-start(f32[64,20,128]{2,1,0:T(8,128)S(1)} %reshape.570) | copy-start | bytes 1966084
  279.1 14.5 %copy-start.53 = (f32[64]{0:T(128)}, f32[64]{0:T(128)S(1)}, u32[]{:S(2)}) copy-start(f32[64]{0:T(128)S(1)} %add_rsqrt_fusion.3) | copy-start | bytes 772
  288.8 3.8 copy-start.11
  288.8 3.8 copy-start.55
  299.4 9.6 %copy-start.7 = (f32[64,20,128]{2,1,0:T(8,128)}, f32[64,20,128]{2,1,0:T(8,128)S(1)}, u32[]{:S(2)}) copy-start(f32[64,20,128]{2,1,0:T(8,128)S(1)} %reshape.572) | copy-start | bytes 1966084
  305.5 3.5 copy-start.59
  315.9 4.5 copy-start.35
  320.4 2.8 copy-start.12
  320.4 2.9 copy-start.40
  320.4 2.9 copy-start.56
  323.2 2.8 copy-start.29
  328.3 9.5 %collective-permute-start.5 = (bf16[64,2560]{1,0:T(8,128)(2,1)}, bf16[64,2560]{1,0:T(8,128)(2,1)}, u32[]{:S(2)}, u32[]{:S(2)}) collective-permute-start(bf16[64,2560]{1,0:T(8,128)(2,1)} %get-tuple-element.28), channel_id=1, source_target_pairs={{1,0},{2,1},{3,2},{5,4},{6,5},{7,6},{9,8},{10,9},{11,10},{13,12},{... | collective-permute-start | bytes 983048 | tf_op jit(solution)/shard_map/ppermute | solution.py:18
  334.8 11.0 %copy-start.5 = (f32[64,20,128]{2,1,0:T(8,128)}, f32[64,20,128]{2,1,0:T(8,128)S(1)}, u32[]{:S(2)}) copy-start(f32[64,20,128]{2,1,0:T(8,128)S(1)} %reshape.574) | copy-start | bytes 1966084
  342.3 3.5 copy-start.60
  352.7 4.4 copy-start.36
  357.1 2.8 copy-start.10
  357.1 2.9 copy-start.41
  357.1 2.9 copy-start.54
  360.0 2.3 copy-start.30
  364.5 15.3 %collective-permute-start.6 = (bf16[64,2560]{1,0:T(8,128)(2,1)}, bf16[64,2560]{1,0:T(8,128)(2,1)}, u32[]{:S(2)}, u32[]{:S(2)}) collective-permute-start(bf16[64,2560]{1,0:T(8,128)(2,1)} %get-tuple-element.26), channel_id=1, source_target_pairs={{1,0},{2,1},{3,2},{5,4},{6,5},{7,6},{9,8},{10,9},{11,10},{13,12},{... | collective-permute-start | bytes 983048 | tf_op jit(solution)/shard_map/ppermute | solution.py:18
  382.7 3.5 copy-start.61
  397.6 2.8 copy-start.8
  397.6 2.8 copy-start.52
  404.9 9.0 %collective-permute-start.7 = (bf16[64,2560]{1,0:T(8,128)(2,1)S(1)}, bf16[64,2560]{1,0:T(8,128)(2,1)S(1)}, u32[]{:S(2)}, u32[]{:S(2)}) collective-permute-start(bf16[64,2560]{1,0:T(8,128)(2,1)S(1)} %get-tuple-element.24), channel_id=1, source_target_pairs={{1,0},{2,1},{3,2},{5,4},{6,5},{7,6},{9,8},{10,9},{11,10},{13,12},{... | collective-permute-start | bytes 983048 | tf_op jit(solution)/shard_map/ppermute | solution.py:18
  431.1 2.8 copy-start.6
  431.1 2.8 copy-start.51
  439.2 2.2 copy-start.38
  444.6 4.4 copy-start.23
  444.6 4.4 copy-start.31
  449.1 2.5 copy-start.3
  449.1 2.5 copy-start.43
  454.2 4.6 copy-start.33
  454.3 4.6 copy-start.34
  467.7 1.8 copy-start.32
  (8 other events, 8.4 us)
Sparse Core Ops, SparseCore 0:
  11.3 85.8 all-gather.1
  467.8 149.5 reduce-scatter.4

commit v3 on v2

--- a/solution.py
+++ b/solution.py
@@ -1,8 +1,11 @@
+import functools
 import math
 
 import jax
 import jax.numpy as jnp
 from jax import lax
+from jax.experimental import pallas as pl
+from jax.experimental.pallas import tpu as pltpu
 from jax.sharding import PartitionSpec as P
 
 FF = 10240
@@ -37,13 +40,52 @@
     )
 
 
+def _panel_kernel(pick_ref, put_ref, panels_ref, blocks_ref, out_ref, *, transpose):
+    out_ref[...] = jnp.zeros_like(out_ref)
+
+    def body(b, carry):
+        source = panels_ref[pick_ref[b]]
+        weight = blocks_ref[b]
+        if transpose:
+            product = lax.dot_general(
+                source, weight, (((1,), (1,)), ((), ())), preferred_element_type=jnp.float32
+            )
+        else:
+            product = jnp.dot(source, weight, preferred_element_type=jnp.float32)
+        target = put_ref[b]
+        out_ref[target] = out_ref[target] + product
+        return carry
+
+    lax.fori_loop(0, blocks_ref.shape[0], body, 0, unroll=True)
+
+
+def panel_kernel(panels, blocks, pick_index, put_index, put_count, transpose):
+    panel_count, rows, width = panels.shape
+    block_count = blocks.shape[0]
+    spec = pltpu.PrefetchScalarGridSpec(
+        num_scalar_prefetch=2,
+        grid=(1,),
+        in_specs=[
+            pl.BlockSpec((panel_count, rows, width), lambda i, *_: (0, 0, 0)),
+            pl.BlockSpec(blocks.shape, lambda i, *_: (0, 0, 0)),
+        ],
+        out_specs=pl.BlockSpec((put_count, rows, width), lambda i, *_: (0, 0, 0)),
+    )
+    cost = pl.CostEstimate(
+        flops=2 * block_count * rows * width * width,
+        transcendentals=0,
+        bytes_accessed=panels.size * 2 + blocks.size * 2 + put_count * rows * width * 4,
+    )
+    return pl.pallas_call(
+        functools.partial(_panel_kernel, transpose=transpose),
+        grid_spec=spec,
+        out_shape=jax.ShapeDtypeStruct((put_count, rows, width), jnp.float32),
+        cost_estimate=cost,
+    )(pick_index, put_index, panels, blocks)
+
+
 def panel_product(panels, blocks, pick_index, put_index, put_count, form):
-    picked = jnp.take(panels, pick_index, axis=0)
-    products = jnp.einsum(form, picked, blocks, preferred_element_type=jnp.float32)
-    placing = (put_index[:, None] == jnp.arange(put_count, dtype=jnp.int32)[None, :]).astype(
-        jnp.float32
-    )
-    return jnp.einsum("brc,bp->prc", products, placing, precision=lax.Precision.HIGH)
+    return panel_kernel(panels, blocks, pick_index, put_index, put_count, form == "bro,bio->bri")
 
 
 def up_product(inputs, gain_row, up_blocks, block_links, hidden_panels, panel_width):

time: 636 us -> 571 us (0.90)
  matrix products: 128 us -> 5.81 us
  Pallas kernels: 0 us -> 93 us
  local copies, waits for them, and re-layouts: 126 us -> 63.3 us
  other arithmetic: 80.1 us -> 110 us
    dot_general x38 -> x0, matrix products: 122 us -> none  [the longest x19 71.2 us: panel_product(): jnp.einsum('brc,bp->prc', products, placing, precision=lax.Precision.HIGH)]
    pallas_call x0 -> x19, Pallas kernels: none -> 93 us  [panel_kernel(): pl.pallas_call(functools.partial(_panel_kernel, transpose=transpose), gri...]
    gather x19 -> x0, local copies, waits for them, and re-layouts: 49 us -> none  [panel_product(): picked = jnp.take(panels, pick_index, axis=0)]
    convert_element_type x9 -> x0, local copies, waits for them, and re-layouts: 12.7 us -> none  [the longest x5 7.03 us: layer_backward(): grad_before = (grad_active * gelu_slope).astype(jnp.bfloat16)]
    convert_element_type x4, other arithmetic: 3.41 us -> 14.6 us  [layer_forward(): active = jax.nn.gelu(before).astype(jnp.bfloat16)]
    reduce_sum x0 -> x5, other arithmetic: none -> 8.68 us  [the longest x4 7.18 us: layer_backward(): gain_grad = jnp.sum(grad_normed * unit_rows, axis=0)]
    all_gather x1, waiting for transfers between devices: 84.3 us -> 76.2 us  [shards(): gathered = lax.all_gather(packed, 'dp', axis=1, tiled=True)[0]]
    ppermute x8, waiting for transfers between devices: 23.9 us -> 30.8 us  [from_behind(): return lax.ppermute(value, axis, pairs)]
  transfers between devices with their start and end apart: 10 -> 10, of which waited for: 8 -> 10; matrix products, arithmetic and copies ran while one was open for 11% -> 6% of each run, Pallas kernels for 0% -> 1%
where the time goes in v3:
time: 571 us; the launch traced here: 562 us
  waiting for transfers between devices  252 us (44%)
  other arithmetic  110 us (19%)
  Pallas kernels  93 us (16%)
  local copies, waits for them, and re-layouts  63.3 us (11%)
  starting transfers between devices  22.5 us (4%)
  between operations  15.1 us (3%)
  matrix products  5.81 us (1%)
    unnamed x3, waiting for transfers between devices  145 us
    pallas_call x19, Pallas kernels, panel_kernel(): pl.pallas_call(functools.partial(_panel_kernel, transpose=transpose), gri...  93 us
    all_gather x1, waiting for transfers between devices, shards(): gathered = lax.all_gather(packed, 'dp', axis=1, tiled=True)[0]  76.2 us
    unnamed x20, other arithmetic  46 us
    unnamed x99, local copies, waits for them, and re-layouts  34.9 us
    ppermute x8, waiting for transfers between devices, from_behind(): return lax.ppermute(value, axis, pairs)  30.8 us
    ppermute x8, starting transfers between devices, from_behind(): return lax.ppermute(value, axis, pairs)  22.4 us
    convert_element_type x4, other arithmetic, layer_forward(): active = jax.nn.gelu(before).astype(jnp.bfloat16)  14.6 us
  transfers between devices with their start and end apart: 10, of which 10 were waited for; matrix products, arithmetic and copies ran while one was open for 6% of the time, Pallas kernels for 1%

profile of v3, /device:TPU:8, one launch (start us, length us, event | category | flops | bytes accessed | tf_op | source)
XLA Modules:
  0.0 562.1 jit_solution(8959002893853205631)
XLA Ops:
  20.9 76.2 %all-gather.2.cloned.1.call-done = bf16[1,64,32896]{2,0,1:T(2,128)(2,1)} async-done(((bf16[1,1,32896]{2,0,1:T(2,128)(2,1)}), bf16[1,64,32896]{2,0,1:T(2,128)(2,1)}) %all-gather.2.cloned.1.call-update) | async-done | bytes 4210704 | tf_op jit(solution)/shard_map/all_gather | solution.py:189
  97.1 3.8 copy.207
  103.0 3.5 copy.111
  107.4 4.7 shard_map.93
  112.1 3.7 fusion.68.panels_ref
  117.6 4.2 shard_map.94
  123.7 3.6 collective-permute-start
  127.4 5.4 shard_map.101
  139.4 4.7 shard_map.95
  144.1 3.7 fusion.76.panels_ref
  147.8 4.3 shard_map.96
  153.4 3.9 collective-permute-start.1
  159.0 5.3 collective-permute-done.1
  166.8 4.7 shard_map.97
  171.5 3.7 fusion.84.panels_ref
  175.1 4.3 shard_map.98
  180.7 3.4 collective-permute-start.2
  185.7 5.0 collective-permute-done.2
  193.2 4.7 shard_map.99
  197.8 3.7 fusion.92.panels_ref
  201.5 4.3 shard_map.100
  207.1 3.6 collective-permute-start.3
  212.3 3.9 collective-permute-done.3
  218.0 2.7 fusion.206
  221.6 4.7 shard_map.102
  226.3 3.7 bitcast_dynamic-update-slice_fusion
  229.9 4.8 bitcast_dynamic-update-slice_fusion.9
  234.8 5.0 shard_map.103
  244.3 3.1 dynamic-slice_convert_fusion
  253.7 2.9 collective-permute-done.4
  257.5 5.3 shard_map.104
  262.8 5.3 bitcast_dynamic-update-slice_fusion.8
  268.1 5.2 shard_map.105
  273.3 2.0 fusion.203
  275.3 2.4 bitcast_dynamic-update-slice_fusion.12
  277.6 2.1 collective-permute-start.5
  282.1 4.7 collective-permute-done.5
  287.6 5.3 shard_map.106
  293.0 5.3 bitcast_dynamic-update-slice_fusion.7
  298.2 5.2 shard_map.107
  303.4 2.2 fusion.200
  305.6 2.3 bitcast_dynamic-update-slice_fusion.11
  311.0 2.2 gather_fusion
  314.1 3.2 collective-permute-done.6
  319.0 5.4 shard_map.108
  324.4 5.2 bitcast_dynamic-update-slice_fusion.6
  329.7 5.2 shard_map.109
  334.8 2.0 fusion.197
  336.8 2.3 bitcast_dynamic-update-slice_fusion.10
  343.7 4.4 collective-permute-done.7
  348.9 5.4 shard_map.110
  354.2 5.5 bitcast_dynamic-update-slice_fusion.5
  359.7 5.2 shard_map.111
  366.4 2.3 constant_dynamic-slice_fusion.3
  368.7 2.3 gather_fusion.1
  371.0 3.2 fusion.136
  374.3 4.3 copy.209
  378.8 3.8 constant_dynamic-slice_fusion.2
  383.7 3.9 gather_fusion.2
  387.6 2.6 fusion.133
  390.2 4.4 copy.208
  394.7 4.1 fusion
  398.8 4.9 copy.115
  407.6 145.1 %reduce-scatter.5.cloned.1.call-done = f32[1,1,264,128]{3,2,1,0:T(8,128)} async-done(((f32[1,64,264,128]{3,2,1,0:T(8,128)}), f32[1,1,264,128]{3,2,1,0:T(8,128)}) %reduce-scatter.5.cloned.1.call-update) | async-done | bytes 135184
  (182 shorter events, 78.0 us)
Async XLA Ops:
  7.2 90.0 %all-gather.2.cloned.1.call-start = ((), (), s32[]{:S(2)}) async-start(), calls=%async_computation.1 | async-start | bytes 8552960 | tf_op jit(solution)/shard_map/all_gather | solution.py:189
  10.2 542.4 %reduce-scatter.5.cloned.1.call-start = ((), (), s32[]{:S(2)}) async-start(), calls=%async_computation.2 | async-start | bytes 8785920
  102.8 3.7 copy-start.7
  102.9 117.7 %copy-start.19 = (f32[2560]{0:T(1024)}, f32[2560]{0:T(1024)S(1)}, u32[]{:S(2)}) copy-start(f32[2560]{0:T(1024)S(1)} %reshape.547) | copy-start | bytes 30724
  123.7 9.1 %copy-start.1 = (f32[80,64,128]{2,1,0:T(8,128)S(1)}, f32[80,64,128]{2,1,0:T(8,128)}, u32[]{:S(2)}) copy-start(f32[80,64,128]{2,1,0:T(8,128)} %shard_map.93) | copy-start | bytes 7864324
  123.7 12.3 %collective-permute-start = (bf16[64,2560]{1,0:T(8,128)(2,1)}, bf16[64,2560]{1,0:T(8,128)(2,1)}, u32[]{:S(2)}, u32[]{:S(2)}) collective-permute-start(bf16[64,2560]{1,0:T(8,128)(2,1)} %fusion.161), channel_id=1, source_target_pairs={{0,1},{1,2},{2,3},{4,5},{5,6},{6,7},{8,9},{9,10},{10,11},{12,13},{... | collective-permute-start | bytes 983048 | tf_op jit(solution)/shard_map/ppermute | solution.py:21
  137.8 0.7 copy-start.12
  147.8 9.5 %copy-start.2 = (f32[80,64,128]{2,1,0:T(8,128)S(1)}, f32[80,64,128]{2,1,0:T(8,128)}, u32[]{:S(2)}) copy-start(f32[80,64,128]{2,1,0:T(8,128)} %shard_map.95) | copy-start | bytes 7864324
  153.4 11.0 %collective-permute-start.1 = (bf16[64,2560]{1,0:T(8,128)(2,1)S(1)}, bf16[64,2560]{1,0:T(8,128)(2,1)S(1)}, u32[]{:S(2)}, u32[]{:S(2)}) collective-permute-start(bf16[64,2560]{1,0:T(8,128)(2,1)S(1)} %fusion.165), channel_id=1, source_target_pairs={{0,1},{1,2},{2,3},{4,5},{5,6},{6,7},{8,9},{9,10},{10,11},{12,13},{... | collective-permute-start | bytes 983048 | tf_op jit(solution)/shard_map/ppermute | solution.py:21
  165.2 0.7 copy-start.13
  175.1 9.0 %copy-start.3 = (f32[80,64,128]{2,1,0:T(8,128)S(1)}, f32[80,64,128]{2,1,0:T(8,128)}, u32[]{:S(2)}) copy-start(f32[80,64,128]{2,1,0:T(8,128)} %shard_map.97) | copy-start | bytes 7864324
  180.7 10.0 %collective-permute-start.2 = (bf16[64,2560]{1,0:T(8,128)(2,1)S(1)}, bf16[64,2560]{1,0:T(8,128)(2,1)S(1)}, u32[]{:S(2)}, u32[]{:S(2)}) collective-permute-start(bf16[64,2560]{1,0:T(8,128)(2,1)S(1)} %fusion.169), channel_id=1, source_target_pairs={{0,1},{1,2},{2,3},{4,5},{5,6},{6,7},{8,9},{9,10},{10,11},{12,13},{... | collective-permute-start | bytes 983048 | tf_op jit(solution)/shard_map/ppermute | solution.py:21
  191.5 0.7 copy-start.14
  201.5 9.2 %copy-start.4 = (f32[80,64,128]{2,1,0:T(8,128)S(1)}, f32[80,64,128]{2,1,0:T(8,128)}, u32[]{:S(2)}) copy-start(f32[80,64,128]{2,1,0:T(8,128)} %shard_map.99) | copy-start | bytes 7864324
  207.1 9.1 %collective-permute-start.3 = (bf16[64,2560]{1,0:T(8,128)(2,1)S(1)}, bf16[64,2560]{1,0:T(8,128)(2,1)S(1)}, u32[]{:S(2)}, u32[]{:S(2)}) collective-permute-start(bf16[64,2560]{1,0:T(8,128)(2,1)S(1)} %fusion.173), channel_id=1, source_target_pairs={{0,1},{1,2},{2,3},{4,5},{5,6},{6,7},{8,9},{9,10},{10,11},{12,13},{... | collective-permute-start | bytes 983048 | tf_op jit(solution)/shard_map/ppermute | solution.py:21
  226.3 3.7 copy-start.6
  239.8 1.1 copy-start.5
  239.9 2.4 copy-start
  239.9 2.4 copy-start.20
  244.3 5.1 copy-start.43
  247.4 2.2 copy-start.42
  247.4 4.1 copy-start.41
  247.5 4.1 copy-start.9
  247.5 9.2 %collective-permute-start.4 = (bf16[64,2560]{1,0:T(8,128)(2,1)}, bf16[64,2560]{1,0:T(8,128)(2,1)S(1)}, u32[]{:S(2)}, u32[]{:S(2)}) collective-permute-start(bf16[64,2560]{1,0:T(8,128)(2,1)} %fusion.157), channel_id=1, source_target_pairs={{1,0},{2,1},{3,2},{5,4},{6,5},{7,6},{9,8},{10,9},{11,10},{13,12},{... | collective-permute-start | bytes 983048 | tf_op jit(solution)/shard_map/ppermute | solution.py:21
  249.6 8.0 %copy-start.8 = (f32[64,20,128]{2,1,0:T(8,128)}, f32[64,20,128]{2,1,0:T(8,128)S(1)}, u32[]{:S(2)}) copy-start(f32[64,20,128]{2,1,0:T(8,128)S(1)} %reshape.552) | copy-start | bytes 1966084
  249.6 1.9 copy-start.34
  251.6 11.3 %copy-start.32 = (f32[64]{0:T(128)}, f32[64]{0:T(128)S(1)}, u32[]{:S(2)}) copy-start(f32[64]{0:T(128)S(1)} %add_rsqrt_fusion.2) | copy-start | bytes 772
  268.1 5.2 copy-start.10
  268.1 7.2 %copy-start.21 = (f32[2560]{0:T(1024)S(1)}, f32[2560]{0:T(1024)}, u32[]{:S(2)}) copy-start(f32[2560]{0:T(1024)} %copy-done.19) | copy-start | bytes 30724
  273.3 6.5 %copy-start.40 = (f32[64]{0:T(128)S(1)}, f32[64]{0:T(128)}, u32[]{:S(2)}) copy-start(f32[64]{0:T(128)} %get-tuple-element.6) | copy-start | bytes 772
  275.3 5.1 copy-start.18
  277.6 9.2 %collective-permute-start.5 = (bf16[64,2560]{1,0:T(8,128)(2,1)}, bf16[64,2560]{1,0:T(8,128)(2,1)S(1)}, u32[]{:S(2)}, u32[]{:S(2)}) collective-permute-start(bf16[64,2560]{1,0:T(8,128)(2,1)} %get-tuple-element.26), channel_id=1, source_target_pairs={{1,0},{2,1},{3,2},{5,4},{6,5},{7,6},{9,8},{10,9},{11,10},{13,12},{... | collective-permute-start | bytes 983048 | tf_op jit(solution)/shard_map/ppermute | solution.py:21
  298.2 5.2 copy-start.35
  298.2 7.4 %copy-start.22 = (f32[2560]{0:T(1024)S(1)}, f32[2560]{0:T(1024)}, u32[]{:S(2)}) copy-start(f32[2560]{0:T(1024)} %copy-done.19) | copy-start | bytes 30724
  307.9 9.3 %collective-permute-start.6 = (bf16[64,2560]{1,0:T(8,128)(2,1)}, bf16[64,2560]{1,0:T(8,128)(2,1)}, u32[]{:S(2)}, u32[]{:S(2)}) collective-permute-start(bf16[64,2560]{1,0:T(8,128)(2,1)} %get-tuple-element.24), channel_id=1, source_target_pairs={{1,0},{2,1},{3,2},{5,4},{6,5},{7,6},{9,8},{10,9},{11,10},{13,12},{... | collective-permute-start | bytes 983048 | tf_op jit(solution)/shard_map/ppermute | solution.py:21
  329.7 5.2 copy-start.33
  329.7 7.2 %copy-start.23 = (f32[2560]{0:T(1024)S(1)}, f32[2560]{0:T(1024)}, u32[]{:S(2)}) copy-start(f32[2560]{0:T(1024)} %copy-done.19) | copy-start | bytes 30724
  339.1 9.0 %collective-permute-start.7 = (bf16[64,2560]{1,0:T(8,128)(2,1)S(1)}, bf16[64,2560]{1,0:T(8,128)(2,1)S(1)}, u32[]{:S(2)}, u32[]{:S(2)}) collective-permute-start(bf16[64,2560]{1,0:T(8,128)(2,1)S(1)} %get-tuple-element.22), channel_id=1, source_target_pairs={{1,0},{2,1},{3,2},{5,4},{6,5},{7,6},{9,8},{10,9},{11,10},{13,12},{... | collective-permute-start | bytes 983048 | tf_op jit(solution)/shard_map/ppermute | solution.py:21
  348.0 6.2 %copy-start.15 = (bf16[64,2560]{1,0:T(8,128)(2,1)}, bf16[64,2560]{1,0:T(8,128)(2,1)S(1)}, u32[]{:S(2)}) copy-start(bf16[64,2560]{1,0:T(8,128)(2,1)S(1)} %collective-permute-done.7) | copy-start | bytes 983044
  359.7 5.2 copy-start.31
  368.7 2.3 copy-start.38
  368.7 2.3 copy-start.39
  374.3 4.3 copy-start.16
  374.3 4.3 copy-start.25
  383.7 3.9 copy-start.36
  383.7 3.9 copy-start.37
  390.2 4.4 copy-start.27
  390.2 4.4 copy-start.28
  390.2 4.4 copy-start.29
  390.2 4.4 copy-start.30
  403.7 1.1 copy-start.11
  403.7 1.2 copy-start.17
  403.7 1.2 copy-start.24
  403.7 1.7 copy-start.26
Sparse Core Ops, SparseCore 0:
  11.2 85.8 all-gather.1
  403.9 148.7 reduce-scatter.4

commit v4 on v3

--- a/solution.py
+++ b/solution.py
@@ -175,24 +175,24 @@
     model_panels = model_width // panel_width
     group_rows = token_rows // MICRO
     block_links = coords[0]
-    block_width = panel_width * panel_width
     gain_count = norm_gains.shape[1]
-    gain_room = -(-gain_count // 128) * 128
+    gain_rows = 16
     packed = jnp.concatenate(
         [
-            up_weights.reshape(1, 1, block_width),
-            down_weights.reshape(1, 1, block_width),
-            jnp.pad(norm_gains.reshape(1, 1, gain_count), ((0, 0), (0, 0), (0, gain_room - gain_count))),
+            up_weights,
+            down_weights,
+            jnp.pad(
+                norm_gains.reshape(1, 1, 1, gain_count),
+                ((0, 0), (0, 0), (0, gain_rows - 1), (0, panel_width - gain_count)),
+            ),
         ],
         axis=2,
     )
     gathered = lax.all_gather(packed, "dp", axis=1, tiled=True)[0]
     block_count = gathered.shape[0]
-    up_blocks = gathered[:, :block_width].reshape(block_count, panel_width, panel_width)
-    down_blocks = gathered[:, block_width : 2 * block_width].reshape(
-        block_count, panel_width, panel_width
-    )
-    gain_row = gathered[:, 2 * block_width : 2 * block_width + gain_count].reshape(-1)
+    up_blocks = gathered[:, :panel_width]
+    down_blocks = gathered[:, panel_width : 2 * panel_width]
+    gain_row = gathered[:, 2 * panel_width, :gain_count].reshape(-1)
     token_groups = tokens.reshape(MICRO, group_rows, model_width)
     cot_groups = cot_groups_of = cotangent.reshape(MICRO, group_rows, model_width)
     last_tick = MICRO + phases - 2
@@ -271,22 +271,14 @@
         preferred_element_type=jnp.float32,
     )
     gain_parts = jnp.pad(
-        gain_total.reshape(block_count, gain_count), ((0, 0), (0, 8 * 128 - gain_count))
-    )
-    totals = jnp.concatenate(
-        [
-            up_total.reshape(block_count, block_width),
-            down_total.reshape(block_count, block_width),
-            gain_parts,
-        ],
-        axis=1,
-    )
-    summed = lax.psum_scatter(
-        totals.reshape(1, block_count, -1, 128), "dp", scatter_dimension=1, tiled=True
-    ).reshape(-1) * grad_scale
-    up_out = summed[:block_width].reshape(1, 1, panel_width, panel_width)
-    down_out = summed[block_width : 2 * block_width].reshape(1, 1, panel_width, panel_width)
-    gain_out = summed[2 * block_width : 2 * block_width + gain_count].reshape(1, gain_count)
+        gain_total.reshape(block_count, 1, gain_count),
+        ((0, 0), (0, 7), (0, panel_width - gain_count)),
+    )
+    totals = jnp.concatenate([up_total, down_total, gain_parts], axis=1)
+    summed = lax.psum_scatter(totals[None], "dp", scatter_dimension=1, tiled=True) * grad_scale
+    up_out = summed[:, :, :panel_width]
+    down_out = summed[:, :, panel_width : 2 * panel_width]
+    gain_out = summed[0, :, 2 * panel_width, :gain_count]
     return (
         up_out,
         down_out,

time: 571 us -> 549 us (0.961)
  local copies, waits for them, and re-layouts: 63.3 us -> 46.3 us
    unnamed x99 -> x50, local copies, waits for them, and re-layouts: 34.9 us -> 10.4 us
    unnamed x20 -> x19, other arithmetic: 46 us -> 42.8 us
where the time goes in v4:
time: 549 us; the launch traced here: 539 us
  waiting for transfers between devices  252 us (46%)
  other arithmetic  108 us (20%)
  Pallas kernels  92 us (17%)
  local copies, waits for them, and re-layouts  46.3 us (8%)
  starting transfers between devices  22.2 us (4%)
  between operations  15 us (3%)
    unnamed x3, waiting for transfers between devices  146 us
    pallas_call x19, Pallas kernels, panel_kernel(): pl.pallas_call(functools.partial(_panel_kernel, transpose=transpose), gri...  92 us
    all_gather x1, waiting for transfers between devices, shards(): gathered = lax.all_gather(packed, 'dp', axis=1, tiled=True)[0]  75.1 us
    unnamed x19, other arithmetic  42.8 us
    ppermute x8, waiting for transfers between devices, from_behind(): return lax.ppermute(value, axis, pairs)  31.2 us
    ppermute x8, starting transfers between devices, from_behind(): return lax.ppermute(value, axis, pairs)  22.1 us
    convert_element_type x4, other arithmetic, layer_forward(): active = jax.nn.gelu(before).astype(jnp.bfloat16)  14.7 us
  transfers between devices with their start and end apart: 10, of which 10 were waited for; matrix products, arithmetic and copies ran while one was open for 6% of the time, Pallas kernels for 1%

profile of v4, /device:TPU:8, one launch (start us, length us, event | category | flops | bytes accessed | tf_op | source)
XLA Modules:
  0.0 538.9 jit_solution(17170783220951659992)
XLA Ops:
  18.1 75.1 %all-gather.2.cloned.1.call-done = bf16[1,64,272,128]{3,2,0,1:T(8,128)(2,1)} async-done(((bf16[1,1,272,128]{3,2,0,1:T(8,128)(2,1)}), bf16[1,64,272,128]{3,2,0,1:T(8,128)(2,1)}) %all-gather.2.cloned.1.call-update) | async-done | bytes 4456464 | tf_op jit(solution)/shard_map/all_gather | solution.py:191
  94.3 4.9 fusion.253
  101.0 4.6 shard_map.93
  105.7 3.7 fusion.68.panels_ref
  109.4 4.2 shard_map.94
  113.5 1.9 fusion.159
  115.5 3.6 collective-permute-start
  119.2 5.3 shard_map.101
  131.2 4.6 shard_map.95
  135.8 3.7 fusion.76.panels_ref
  139.5 4.3 shard_map.96
  145.0 3.4 collective-permute-start.1
  150.2 5.8 %collective-permute-done.1 = bf16[64,2560]{1,0:T(8,128)(2,1)S(1)} collective-permute-done((bf16[64,2560]{1,0:T(8,128)(2,1)S(1)}, bf16[64,2560]{1,0:T(8,128)(2,1)S(1)}, u32[]{:S(2)}, u32[]{:S(2)}) %collective-permute-start.1) | collective-permute-done | bytes 327712 | tf_op jit(solution)/shard_map/ppermute | solution.py:21
  158.5 4.6 shard_map.97
  163.1 3.7 fusion.84.panels_ref
  166.7 4.3 shard_map.98
  172.3 3.6 collective-permute-start.2
  177.6 4.8 collective-permute-done.2
  184.8 4.6 shard_map.99
  189.4 3.7 fusion.92.panels_ref
  193.1 4.3 shard_map.100
  198.7 3.4 collective-permute-start.3
  203.8 4.0 collective-permute-done.3
  209.6 2.0 fusion.204
  212.5 4.6 shard_map.102
  217.1 3.7 bitcast_dynamic-update-slice_fusion
  220.9 4.8 bitcast_dynamic-update-slice_fusion.9
  225.7 5.0 shard_map.103
  232.7 1.9 fusion.155
  234.7 3.0 dynamic-slice_convert_fusion
  237.8 2.1 collective-permute-start.4
  244.2 2.8 collective-permute-done.4
  247.8 5.3 shard_map.104
  253.1 5.3 bitcast_dynamic-update-slice_fusion.8
  258.4 5.0 shard_map.105
  265.0 2.2 bitcast_dynamic-update-slice_fusion.12
  267.2 1.9 collective-permute-start.5
  271.3 4.8 collective-permute-done.5
  276.9 5.3 shard_map.106
  282.3 5.3 bitcast_dynamic-update-slice_fusion.7
  287.5 5.0 shard_map.107
  294.1 2.3 bitcast_dynamic-update-slice_fusion.11
  296.4 2.2 collective-permute-start.6
  300.7 1.8 fusion.235
  302.5 3.2 collective-permute-done.6
  305.7 1.8 bitcast_bitcast_fusion.3.panels_ref
  307.5 5.3 shard_map.108
  312.8 5.4 bitcast_dynamic-update-slice_fusion.6
  318.2 5.0 shard_map.109
  325.0 2.3 bitcast_dynamic-update-slice_fusion.10
  327.3 1.9 collective-permute-start.7
  330.1 1.8 fusion.233
  331.9 4.4 collective-permute-done.7
  337.1 5.3 shard_map.110
  342.4 5.3 bitcast_dynamic-update-slice_fusion.5
  347.7 5.0 shard_map.111
  354.5 4.0 constant_dynamic-slice_fusion.3
  358.7 3.8 constant_dynamic-slice_fusion.2
  362.6 3.9 gather_fusion.1
  366.5 2.1 gather_fusion.3
  368.6 3.9 gather_fusion.2
  372.6 2.7 convolution_bitcast_fusion.1
  376.4 3.6 fusion
  383.9 145.6 %reduce-scatter.5.cloned.1.call-done = f32[1,1,264,128]{3,2,1,0:T(8,128)} async-done(((f32[1,64,264,128]{3,2,1,0:T(8,128)}), f32[1,1,264,128]{3,2,1,0:T(8,128)}) %reduce-scatter.5.cloned.1.call-update) | async-done | bytes 135184
  (133 shorter events, 64.9 us)
Async XLA Ops:
  7.2 86.1 %all-gather.2.cloned.1.call-start = ((), (), s32[]{:S(2)}) async-start(), calls=%async_computation.1 | async-start | bytes 4526080 | tf_op jit(solution)/shard_map/all_gather | solution.py:191
  9.3 520.2 %reduce-scatter.5.cloned.1.call-start = ((), (), s32[]{:S(2)}) async-start(), calls=%async_computation.2 | async-start | bytes 8785920
  94.2 5.9 %copy-start.7 = (bf16[128,2560]{1,0:T(8,128)(2,1)S(1)}, bf16[128,2560]{1,0:T(8,128)(2,1)}, u32[]{:S(2)}) copy-start(bf16[128,2560]{1,0:T(8,128)(2,1)} %param.10) | copy-start | bytes 1966084
  115.4 9.1 %copy-start.1 = (f32[80,64,128]{2,1,0:T(8,128)S(1)}, f32[80,64,128]{2,1,0:T(8,128)}, u32[]{:S(2)}) copy-start(f32[80,64,128]{2,1,0:T(8,128)} %shard_map.93) | copy-start | bytes 7864324
  115.5 12.3 %collective-permute-start = (bf16[64,2560]{1,0:T(8,128)(2,1)}, bf16[64,2560]{1,0:T(8,128)(2,1)}, u32[]{:S(2)}, u32[]{:S(2)}) collective-permute-start(bf16[64,2560]{1,0:T(8,128)(2,1)} %fusion.159), channel_id=1, source_target_pairs={{0,1},{1,2},{2,3},{4,5},{5,6},{6,7},{8,9},{9,10},{10,11},{12,13},{... | collective-permute-start | bytes 983048 | tf_op jit(solution)/shard_map/ppermute | solution.py:21
  129.5 0.7 copy-start.13
  139.5 9.0 %copy-start.2 = (f32[80,64,128]{2,1,0:T(8,128)S(1)}, f32[80,64,128]{2,1,0:T(8,128)}, u32[]{:S(2)}) copy-start(f32[80,64,128]{2,1,0:T(8,128)} %shard_map.95) | copy-start | bytes 7864324
  145.0 10.9 %collective-permute-start.1 = (bf16[64,2560]{1,0:T(8,128)(2,1)S(1)}, bf16[64,2560]{1,0:T(8,128)(2,1)S(1)}, u32[]{:S(2)}, u32[]{:S(2)}) collective-permute-start(bf16[64,2560]{1,0:T(8,128)(2,1)S(1)} %fusion.163), channel_id=1, source_target_pairs={{0,1},{1,2},{2,3},{4,5},{5,6},{6,7},{8,9},{9,10},{10,11},{12,13},{... | collective-permute-start | bytes 983048 | tf_op jit(solution)/shard_map/ppermute | solution.py:21
  156.8 0.7 copy-start.14
  166.7 9.1 %copy-start.3 = (f32[80,64,128]{2,1,0:T(8,128)S(1)}, f32[80,64,128]{2,1,0:T(8,128)}, u32[]{:S(2)}) copy-start(f32[80,64,128]{2,1,0:T(8,128)} %shard_map.97) | copy-start | bytes 7864324
  172.3 10.0 %collective-permute-start.2 = (bf16[64,2560]{1,0:T(8,128)(2,1)S(1)}, bf16[64,2560]{1,0:T(8,128)(2,1)S(1)}, u32[]{:S(2)}, u32[]{:S(2)}) collective-permute-start(bf16[64,2560]{1,0:T(8,128)(2,1)S(1)} %fusion.167), channel_id=1, source_target_pairs={{0,1},{1,2},{2,3},{4,5},{5,6},{6,7},{8,9},{9,10},{10,11},{12,13},{... | collective-permute-start | bytes 983048 | tf_op jit(solution)/shard_map/ppermute | solution.py:21
  183.2 0.7 copy-start.15
  193.1 9.0 %copy-start.4 = (f32[80,64,128]{2,1,0:T(8,128)S(1)}, f32[80,64,128]{2,1,0:T(8,128)}, u32[]{:S(2)}) copy-start(f32[80,64,128]{2,1,0:T(8,128)} %shard_map.99) | copy-start | bytes 7864324
  198.7 9.1 %collective-permute-start.3 = (bf16[64,2560]{1,0:T(8,128)(2,1)S(1)}, bf16[64,2560]{1,0:T(8,128)(2,1)S(1)}, u32[]{:S(2)}, u32[]{:S(2)}) collective-permute-start(bf16[64,2560]{1,0:T(8,128)(2,1)S(1)} %fusion.171), channel_id=1, source_target_pairs={{0,1},{1,2},{2,3},{4,5},{5,6},{6,7},{8,9},{9,10},{10,11},{12,13},{... | collective-permute-start | bytes 983048 | tf_op jit(solution)/shard_map/ppermute | solution.py:21
  217.1 3.7 copy-start.6
  230.7 1.1 copy-start.5
  230.8 1.9 copy-start
  237.8 9.2 %collective-permute-start.4 = (bf16[64,2560]{1,0:T(8,128)(2,1)}, bf16[64,2560]{1,0:T(8,128)(2,1)S(1)}, u32[]{:S(2)}, u32[]{:S(2)}) collective-permute-start(bf16[64,2560]{1,0:T(8,128)(2,1)} %fusion.155), channel_id=1, source_target_pairs={{1,0},{2,1},{3,2},{5,4},{6,5},{7,6},{9,8},{10,9},{11,10},{13,12},{... | collective-permute-start | bytes 983048 | tf_op jit(solution)/shard_map/ppermute | solution.py:21
  243.2 9.9 %copy-start.11 = (f32[64,20,128]{2,1,0:T(8,128)}, f32[64,20,128]{2,1,0:T(8,128)S(1)}, u32[]{:S(2)}) copy-start(f32[64,20,128]{2,1,0:T(8,128)S(1)} %reshape.569) | copy-start | bytes 1966084
  247.0 18.0 %copy-start.18 = (bf16[64,2560]{1,0:T(8,128)(2,1)}, bf16[64,2560]{1,0:T(8,128)(2,1)S(1)}, u32[]{:S(2)}) copy-start(bf16[64,2560]{1,0:T(8,128)(2,1)S(1)} %collective-permute-done.4) | copy-start | bytes 983044
  267.2 9.0 %collective-permute-start.5 = (bf16[64,2560]{1,0:T(8,128)(2,1)S(1)}, bf16[64,2560]{1,0:T(8,128)(2,1)S(1)}, u32[]{:S(2)}, u32[]{:S(2)}) collective-permute-start(bf16[64,2560]{1,0:T(8,128)(2,1)S(1)} %get-tuple-element.26), channel_id=1, source_target_pairs={{1,0},{2,1},{3,2},{5,4},{6,5},{7,6},{9,8},{10,9},{11,10},{13,12},{... | collective-permute-start | bytes 983048 | tf_op jit(solution)/shard_map/ppermute | solution.py:21
  270.3 12.0 %copy-start.10 = (f32[64,20,128]{2,1,0:T(8,128)}, f32[64,20,128]{2,1,0:T(8,128)S(1)}, u32[]{:S(2)}) copy-start(f32[64,20,128]{2,1,0:T(8,128)S(1)} %reshape.571) | copy-start | bytes 1966084
  276.1 18.0 %copy-start.19 = (bf16[64,2560]{1,0:T(8,128)(2,1)}, bf16[64,2560]{1,0:T(8,128)(2,1)S(1)}, u32[]{:S(2)}) copy-start(bf16[64,2560]{1,0:T(8,128)(2,1)S(1)} %collective-permute-done.5) | copy-start | bytes 983044
  296.4 9.3 %collective-permute-start.6 = (bf16[64,2560]{1,0:T(8,128)(2,1)}, bf16[64,2560]{1,0:T(8,128)(2,1)}, u32[]{:S(2)}, u32[]{:S(2)}) collective-permute-start(bf16[64,2560]{1,0:T(8,128)(2,1)} %get-tuple-element.24), channel_id=1, source_target_pairs={{1,0},{2,1},{3,2},{5,4},{6,5},{7,6},{9,8},{10,9},{11,10},{13,12},{... | collective-permute-start | bytes 983048 | tf_op jit(solution)/shard_map/ppermute | solution.py:21
  323.2 6.0 %copy-start.20 = (bf16[64,2560]{1,0:T(8,128)(2,1)S(1)}, bf16[64,2560]{1,0:T(8,128)(2,1)}, u32[]{:S(2)}) copy-start(bf16[64,2560]{1,0:T(8,128)(2,1)} %copy-done.19) | copy-start | bytes 983044
  327.3 9.0 %collective-permute-start.7 = (bf16[64,2560]{1,0:T(8,128)(2,1)S(1)}, bf16[64,2560]{1,0:T(8,128)(2,1)S(1)}, u32[]{:S(2)}, u32[]{:S(2)}) collective-permute-start(bf16[64,2560]{1,0:T(8,128)(2,1)S(1)} %get-tuple-element.22), channel_id=1, source_target_pairs={{1,0},{2,1},{3,2},{5,4},{6,5},{7,6},{9,8},{10,9},{11,10},{13,12},{... | collective-permute-start | bytes 983048 | tf_op jit(solution)/shard_map/ppermute | solution.py:21
  336.3 22.2 %copy-start.16 = (bf16[64,2560]{1,0:T(8,128)(2,1)}, bf16[64,2560]{1,0:T(8,128)(2,1)S(1)}, u32[]{:S(2)}) copy-start(bf16[64,2560]{1,0:T(8,128)(2,1)S(1)} %collective-permute-done.7) | copy-start | bytes 983044
  354.5 4.0 copy-start.21
  372.6 2.8 copy-start.8
  372.6 2.9 copy-start.9
  380.1 1.1 copy-start.12
  380.1 1.2 copy-start.17
  380.1 1.7 copy-start.22
Sparse Core Ops, SparseCore 0:
  11.3 81.9 all-gather.1
  380.2 149.2 reduce-scatter.4
